TPU v7x, 512 devices: a whole 4x8x8 slice. The times are simulated.
512 devices in a mesh: req: 64 (over x, z, core), ch: 8 (over y).
Axes of the slice: x: 4, y: 8, z: 8, core: 2. Of those that a mesh axis runs over, the one named last changes fastest.
Arguments:
- tokens: bfloat16 [128, 4096], P('req', 'ch'), may hold values from -80 to 80
- attn_gain: float32 [4096], P('ch'), may hold values from 0.1 to 1.9
- w_query: bfloat16 [4096, 4096], P('ch', 'req'), may hold values from -0.09375 to 0.09375
- w_keyval: bfloat16 [4096, 512], P('ch', 'req'), may hold values from -0.09375 to 0.09375
- cache: bfloat16 [2, 128, 256, 2048], P(None, 'req', 'ch'), may hold values from -70 to 70
- lengths: int32 [128], P('req'), may hold values from 1 to 2047, as said below
- write_pos: int32 [128], P('req'), may hold values from 0 to 2047
- w_out: bfloat16 [4096, 4096], P('ch', 'req'), may hold values from -0.09375 to 0.09375
- mlp_gain: float32 [4096], P('ch'), may hold values from 0.1 to 1.9
- w_gate_up: bfloat16 [4096, 24576], P('ch', 'req'), may hold values from -0.09375 to 0.09375
- w_down: bfloat16 [12288, 4096], P('req', 'ch'), may hold values from -0.0546875 to 0.0546875
Outputs:
- layer_out: bfloat16 [128, 4096], P('req', 'ch')
- kv_new: bfloat16 [128, 512], P('req', 'ch')
Inputs may be any that keep to these rules, and one draw needn't show every extreme that they name: lengths[b] earlier tokens of request b are in the cache; the largest equals 2047 in every draw. The new token of request b goes to slot write_pos[b]; its earlier tokens fill the slots before it, going back cyclically.
All inputs are finite; a program needn't handle non-finite values.
Results may differ from a plain program's by a relative error of at most 0.0064.
Values may be sent and summed in bfloat16 or wider, within the bound.
No kernel may reach another device: no remote copies, remote signals or barrier semaphores. Data moves between devices by JAX's collectives and lax.ppermute only.
A program may use at most 64 MiB of HBM per device.

v0:
```python
import math

import jax
import jax.numpy as jnp
from jax import lax
from jax.sharding import PartitionSpec as P

D = 4096
H = 16
HD = 256


EPSILON = 1e-06


def rms_norm(values, gain):
    wide = values.astype(jnp.float32)
    squares = jnp.sum(wide * wide, axis=1)
    summed = lax.psum(squares, "ch")
    meansq = summed / D
    return (wide * lax.rsqrt(meansq + EPSILON)[:, None] * gain[None, :]).astype(jnp.bfloat16)


def body(
    tokens,
    attn_gain,
    w_query,
    w_keyval,
    cache,
    lengths,
    write_pos,
    w_out,
    mlp_gain,
    w_gate_up,
    w_down,
):
    rows = tokens.shape[0]
    chan = cache.shape[2]
    window = cache.shape[3]
    factor = 1.0 / math.sqrt(HD)
    normed = rms_norm(tokens, attn_gain)
    joined = jnp.concatenate([w_query, w_keyval], axis=1)
    head_parts = jnp.dot(
        lax.all_gather(normed, "req", axis=0, tiled=True),
        joined,
        preferred_element_type=jnp.float32,
    )
    query_cols = w_query.shape[1]
    query_part, keyval_part = (
        lax.all_to_all(head_parts[:, :query_cols], "req", split_axis=0, concat_axis=1, tiled=True),
        lax.all_to_all(head_parts[:, query_cols:], "req", split_axis=0, concat_axis=1, tiled=True),
    )
    query_sum, keyval_sum = (
        lax.psum_scatter(query_part, "ch", scatter_dimension=1, tiled=True),
        lax.psum_scatter(keyval_part, "ch", scatter_dimension=1, tiled=True),
    )
    queries = query_sum.astype(jnp.bfloat16).reshape(rows, H, chan)
    keyval_new = keyval_sum.astype(jnp.bfloat16)
    key_new = keyval_new[:, :chan]
    value_new = keyval_new[:, chan:]
    keys = cache[0]
    values_cache = cache[1]
    own_part = jnp.sum(
        queries.astype(jnp.float32) * key_new.astype(jnp.float32)[:, None, :], axis=-1
    )
    score_part = jnp.einsum("bhe,bew->bhw", queries, keys, preferred_element_type=jnp.float32)
    summed, own_sum = lax.psum((score_part, own_part), "ch")
    slot_index = jnp.arange(window, dtype=jnp.int32)
    offset = (write_pos[:, None] - 1 - slot_index[None, :]) % window
    usable = offset < lengths[:, None]
    scores = jnp.where(usable[:, None, :], summed * factor, -jnp.inf)
    own_score = own_sum * factor
    top = jnp.maximum(jnp.max(scores, axis=-1), own_score)
    weights = jnp.exp(scores - top[..., None])
    own_weight = jnp.exp(own_score - top)
    total = jnp.sum(weights, axis=-1) + own_weight
    weights_low = weights.astype(jnp.bfloat16)
    numer = jnp.einsum(
        "bhw,bew->bhe", weights_low, values_cache, preferred_element_type=jnp.float32
    )
    numer = (
        numer
        + own_weight.astype(jnp.bfloat16).astype(jnp.float32)[..., None]
        * value_new.astype(jnp.float32)[:, None, :]
    )
    attn_local = (numer / total[..., None]).astype(jnp.bfloat16).reshape(rows, H * chan)
    out_parts = jnp.dot(
        lax.all_gather(attn_local, "req", axis=0, tiled=True),
        w_out,
        preferred_element_type=jnp.float32,
    )
    out_part = lax.all_to_all(out_parts, "req", split_axis=0, concat_axis=1, tiled=True)
    out_sum = lax.psum_scatter(out_part, "ch", scatter_dimension=1, tiled=True)
    first = (tokens.astype(jnp.float32) + out_sum).astype(jnp.bfloat16)
    normed_two = rms_norm(first, mlp_gain)
    hidden_cols = w_gate_up.shape[1] // 2
    ffn_parts = jnp.dot(
        lax.all_gather(normed_two, "req", axis=0, tiled=True),
        w_gate_up,
        preferred_element_type=jnp.float32,
    )
    ffn_total = lax.psum(ffn_parts, "ch")
    hidden = (
        jax.nn.gelu(ffn_total[:, :hidden_cols], approximate=True) * ffn_total[:, hidden_cols:]
    ).astype(jnp.bfloat16)
    down_sum = lax.psum_scatter(
        jnp.dot(hidden, w_down, preferred_element_type=jnp.float32),
        "req",
        scatter_dimension=0,
        tiled=True,
    )
    layer_out = (first.astype(jnp.float32) + down_sum).astype(jnp.bfloat16)
    return (layer_out, keyval_new)


def solution(mesh):
    placed = (
        P("req", "ch"),
        P("ch"),
        P("ch", "req"),
        P("ch", "req"),
        P(None, "req", "ch", None),
        P("req"),
        P("req"),
        P("ch", "req"),
        P("ch"),
        P("ch", "req"),
        P("req", "ch"),
    )
    return jax.shard_map(
        body,
        mesh=mesh,
        in_specs=placed,
        out_specs=(P("req", "ch"), P("req", "ch")),
        check_vma=False,
    )
```

profile of v0, /device:TPU:1, one launch (start us, length us, event | category | flops | bytes accessed | tf_op | source)
XLA Modules:
  0.0 728.1 jit_solution(11447148937282177522)
XLA Ops:
  7.2 0.8 fusion.36
  8.0 14.7 %psum.35 = f32[2]{0:T(128)S(1)} all-reduce(f32[2]{0:T(128)S(1)} %fusion.36), channel_id=1, replica_groups=mesh['req'=64,'ch'=8] {'ch'}, use_global_device_ids=true, to_apply=%region_1.0 | all-reduce | flops 2 | bytes 16 | tf_op jit(solution)/shard_map/psum | solution.py:19
  22.7 0.8 fusion.45
  23.5 60.2 %all-gather = bf16[64,2,512]{2,1,0:T(2,128)(2,1)S(1)} all-gather(bf16[1,2,512]{2,1,0:T(2,128)(2,1)S(1)} %fusion.45), channel_id=1, replica_groups=mesh['req'=64,'ch'=8] {'req'}, dimensions={0}, use_global_device_ids=true | all-gather | bytes 133120 | tf_op jit(solution)/shard_map/all_gather | solution.py:44
  83.7 1.0 fusion.24
  84.8 0.7 copy.28
  85.5 5.6 all-to-all-start.1
  91.1 0.1 copy.26
  91.2 0.7 reshape.85
  91.9 8.9 %all-to-all-done.1 = f32[64,2,8]{2,1,0:T(2,128)S(1)} async-done(((f32[64,2,8]{2,1,0:T(2,128)}), f32[64,2,8]{2,1,0:T(2,128)S(1)}, u32[]{:S(2)}, u32[]{:S(2)}) %all-to-all-start.1) | async-done | bytes 4128 | tf_op jit(solution)/shard_map/all_to_all | solution.py:51
  100.8 4.4 all-to-all-start
  105.2 1.2 copy.40
  106.5 0.7 broadcast_add_fusion
  107.2 7.5 %all-to-all-done = f32[64,1,128]{2,1,0:T(1,128)S(1)} async-done(((f32[64,1,128]{2,1,0:T(1,128)}), f32[64,1,128]{2,1,0:T(1,128)S(1)}, u32[]{:S(2)}, u32[]{:S(2)}) %all-to-all-start) | async-done | bytes 32800 | tf_op jit(solution)/shard_map/all_to_all | solution.py:50
  114.6 0.5 broadcast.73
  115.1 0.7 reduce
  115.9 0.1 reshape.86
  116.0 2.0 copy.39
  118.1 0.1 fusion.35
  118.2 23.1 %reduce-scatter.12.cloned.1.call-done = f32[64,2]{1,0:T(8,128)} async-done(((f32[512,2]{1,0:T(8,128)}), f32[64,2]{1,0:T(8,128)}) %reduce-scatter.12.cloned.1.call-update) | async-done | bytes 528
  141.3 0.8 copy.36
  142.2 47.1 %reduce-scatter.10.cloned.1.call-done = f32[512,2]{1,0:T(8,128)} async-done(((f32[4096,2]{1,0:T(8,128)}), f32[512,2]{1,0:T(8,128)}) %reduce-scatter.10.cloned.1.call-update) | async-done | bytes 4112
  189.3 1.1 copy.34
  190.5 0.9 fusion.3
  191.6 11.9 %psum.37 = f32[2,16]{1,0:T(2,128)S(1)} all-reduce(f32[2,16]{1,0:T(2,128)S(1)} %multiply_reduce_fusion), channel_id=1, replica_groups=mesh['req'=64,'ch'=8] {'ch'}, use_global_device_ids=true, to_apply=%region_7.8 | all-reduce | flops 32 | bytes 256 | tf_op jit(solution)/shard_map/psum | solution.py:67
  203.5 64.4 %all-reduce.5.cloned.1.call-done = f32[2,16,2048]{2,1,0:T(8,128)} async-done(((f32[2,16,2048]{2,1,0:T(8,128)}), f32[2,16,2048]{2,1,0:T(8,128)}) %all-reduce.5.cloned.1.call-update) | async-done | bytes 262160 | tf_op jit(solution)/shard_map/psum | solution.py:67
  267.9 1.1 fusion.7
  269.0 1.2 fusion.8
  270.1 1.2 fusion.1
  271.4 0.1 reshape.73
  271.4 57.0 %all-gather.1 = bf16[64,2,512]{2,1,0:T(2,128)(2,1)S(1)} all-gather(bf16[1,2,512]{2,1,0:T(2,128)(2,1)S(1)} %reshape.73), channel_id=1, replica_groups=mesh['req'=64,'ch'=8] {'req'}, dimensions={0}, use_global_device_ids=true | all-gather | bytes 133120 | tf_op jit(solution)/shard_map/all_gather | solution.py:88
  328.5 0.2 fusion.55
  328.7 0.1 reshape.87
  328.8 16.1 %all_to_all.57 = f32[64,1,128]{2,1,0:T(1,128)S(1)} all-to-all(f32[64,1,128]{2,1,0:T(1,128)S(1)} %reshape.87), channel_id=1, replica_groups=mesh['req'=64,'ch'=8] {'req'}, dimensions={0} | all-to-all | bytes 65536 | tf_op jit(solution)/shard_map/all_to_all | solution.py:92
  344.9 0.7 reduce.1
  345.6 0.1 reshape.88
  345.8 2.0 copy.41
  347.9 32.4 %reduce-scatter.14.cloned.1.call-done = f32[512,2]{1,0:T(8,128)} async-done(((f32[4096,2]{1,0:T(8,128)}), f32[512,2]{1,0:T(8,128)}) %reduce-scatter.14.cloned.1.call-update) | async-done | bytes 4112
  380.3 1.1 copy.38
  381.4 0.1 fusion.40
  381.5 12.0 %psum.38 = f32[2]{0:T(128)S(1)} all-reduce(f32[2]{0:T(128)S(1)} %get-tuple-element.2), channel_id=1, replica_groups=mesh['req'=64,'ch'=8] {'ch'}, use_global_device_ids=true, to_apply=%region_11.12 | all-reduce | flops 2 | bytes 16 | tf_op jit(solution)/shard_map/psum | solution.py:19
  393.6 59.6 %all-gather.2 = bf16[64,2,512]{2,1,0:T(2,128)(2,1)S(1)} all-gather(bf16[1,2,512]{2,1,0:T(2,128)(2,1)S(1)} %fusion.44), channel_id=1, replica_groups=mesh['req'=64,'ch'=8] {'req'}, dimensions={0}, use_global_device_ids=true | all-gather | bytes 133120 | tf_op jit(solution)/shard_map/all_gather | solution.py:98
  453.2 0.9 fusion.56
  454.2 69.2 %all-reduce.7.cloned.1.call-done = f32[128,384]{1,0:T(8,128)} async-done(((f32[128,384]{1,0:T(8,128)}), f32[128,384]{1,0:T(8,128)}) %all-reduce.7.cloned.1.call-update) | async-done | bytes 196624 | tf_op jit(solution)/shard_map/psum | solution.py:102
  523.4 1.9 fusion.28
  525.3 1.3 dynamic-slice
  527.3 192.7 %all-reduce.9.cloned.1.call-done = f32[128,512]{1,0:T(8,128)} async-done(((f32[128,512]{1,0:T(8,128)}), f32[128,512]{1,0:T(8,128)}) %all-reduce.9.cloned.1.call-update) | async-done | bytes 262160
  720.0 1.3 fusion.43
  (41 shorter events, 0.9 us)
Async XLA Ops:
  7.2 446.1 %copy-start = (bf16[512,384]{1,0:T(8,128)(2,1)S(1)}, bf16[512,384]{1,0:T(8,128)(2,1)}, u32[]{:S(2)}) copy-start(bf16[512,384]{1,0:T(8,128)(2,1)} %param.20) | copy-start | bytes 1179652
  85.5 15.3 %all-to-all-start.1 = ((f32[64,2,8]{2,1,0:T(2,128)}), f32[64,2,8]{2,1,0:T(2,128)S(1)}, u32[]{:S(2)}, u32[]{:S(2)}) async-start(f32[64,2,8]{2,1,0:T(2,128)} %bitcast.4), calls=%async_computation.1 | async-start | bytes 131072 | tf_op jit(solution)/shard_map/all_to_all | solution.py:51
  100.8 13.8 %all-to-all-start = ((f32[64,1,128]{2,1,0:T(1,128)}), f32[64,1,128]{2,1,0:T(1,128)S(1)}, u32[]{:S(2)}, u32[]{:S(2)}) async-start(f32[64,1,128]{2,1,0:T(1,128)} %reshape.85), calls=%async_computation | async-start | bytes 65536 | tf_op jit(solution)/shard_map/all_to_all | solution.py:50
  105.2 36.1 %reduce-scatter.12.cloned.1.call-start = ((), (), s32[]{:S(2)}) async-start(), calls=%async_computation.9 | async-start | bytes 294912
  106.4 82.9 %reduce-scatter.10.cloned.1.call-start = ((), (), s32[]{:S(2)}) async-start(), calls=%async_computation.8 | async-start | bytes 2359296
  116.0 2.2 copy-start.7
  116.0 74.5 %copy-start.2 = (bf16[2,2,32,2048]{3,2,1,0:T(8,128)(2,1)S(1)}, bf16[2,2,32,2048]{3,2,1,0:T(8,128)(2,1)}, u32[]{:S(2)}) copy-start(bf16[2,2,32,2048]{3,2,1,0:T(8,128)(2,1)} %param.15) | copy-start | bytes 1572868
  118.0 210.5 %copy-start.3 = (bf16[512,64]{0,1:T(8,128)(2,1)S(1)}, bf16[512,64]{0,1:T(8,128)(2,1)}, u32[]{:S(2)}) copy-start(bf16[512,64]{0,1:T(8,128)(2,1)} %param.18) | copy-start | bytes 196612
  118.1 149.8 %all-reduce.5.cloned.1.call-start = ((), (), s32[]{:S(2)}) async-start(), calls=%async_computation.6 | async-start | bytes 524288 | tf_op jit(solution)/shard_map/psum | solution.py:67
  142.2 205.6 %copy-start.5 = (bf16[2,64]{1,0:T(2,128)(2,1)}, bf16[2,64]{1,0:T(2,128)(2,1)S(1)}, u32[]{:S(2)}) copy-start(bf16[2,64]{1,0:T(2,128)(2,1)S(1)} %copy.36) | copy-start | bytes 772
  191.4 188.9 %reduce-scatter.14.cloned.1.call-start = ((), (), s32[]{:S(2)}) async-start(), calls=%async_computation.10 | async-start | bytes 2359296
  345.7 35.6 %copy-start.4 = (bf16[2,512]{1,0:T(2,128)(2,1)S(1)}, bf16[2,512]{1,0:T(2,128)(2,1)}, u32[]{:S(2)}) copy-start(bf16[2,512]{1,0:T(2,128)(2,1)} %param.11) | copy-start | bytes 6148
  345.8 47.8 %copy-start.6 = (f32[512]{0:T(512)S(1)}, f32[512]{0:T(512)}, u32[]{:S(2)}) copy-start(f32[512]{0:T(512)} %param.19) | copy-start | bytes 6148
  347.8 175.6 %copy-start.1 = (bf16[192,512]{1,0:T(8,128)(2,1)S(1)}, bf16[192,512]{1,0:T(8,128)(2,1)}, u32[]{:S(2)}) copy-start(bf16[192,512]{1,0:T(8,128)(2,1)} %param.21) | copy-start | bytes 589828
  347.8 175.6 %all-reduce.7.cloned.1.call-start = ((), (), s32[]{:S(2)}) async-start(), calls=%async_computation.7 | async-start | bytes 393216 | tf_op jit(solution)/shard_map/psum | solution.py:102
  454.2 265.8 %all-reduce.9.cloned.1.call-start = ((), (), s32[]{:S(2)}) async-start(), calls=%async_computation.11 | async-start | bytes 524288
Sparse Core Ops, SparseCore 0:
  108.8 32.4 reduce-scatter.11
  144.2 45.0 reduce-scatter.9
  191.6 76.2 all-reduce.4
  348.0 32.2 reduce-scatter.13
  454.3 69.0 all-reduce.6
  526.7 193.2 all-reduce.8
where the time goes:
time: 729 us; the launch traced here: 728 us
  waiting for transfers between devices  446 us (61%)
  blocking collectives  231 us (32%)
  between operations  15 us (2%)
  local copies, waits for them, and re-layouts  12.2 us (2%)
  starting transfers between devices  10.2 us (1%)
  other arithmetic  7.74 us (1%)
    unnamed x10, waiting for transfers between devices  295 us
    psum x1, waiting for transfers between devices, body(): ffn_total = lax.psum(ffn_parts, 'ch')  69.2 us
    psum x1, waiting for transfers between devices, body(): summed, own_sum = lax.psum((score_part, own_part), 'ch')  64.4 us
    all_gather x1, blocking collectives, body(): lax.all_gather(normed, 'req', axis=0, tiled=True)  60.2 us
    all_gather x1, blocking collectives, body(): lax.all_gather(normed_two, 'req', axis=0, tiled=True)  59.6 us
    all_gather x1, blocking collectives, body(): lax.all_gather(attn_local, 'req', axis=0, tiled=True)  57 us
    psum x2, blocking collectives, rms_norm(): summed = lax.psum(squares, 'ch')  26.7 us
    all_to_all x1, blocking collectives, body(): lax.all_to_all(out_parts, 'req', split_axis=0, concat_axis=1, tiled=True)  16.1 us
  transfers between devices with their start and end apart: 8, of which 8 were waited for; matrix products, arithmetic and copies ran while one was open for 1% of the time, Pallas kernels for 0%

commit v1 on v0

v1 whole, which is shorter than its diff:
```python
import math

import jax
import jax.numpy as jnp
from jax import lax
from jax.sharding import PartitionSpec as P

D = 4096
H = 16
HD = 256


EPSILON = 1e-06


def gather_rows(x, axis, n):
    return lax.all_to_all(jnp.broadcast_to(x[None], (n,) + x.shape), axis, 0, 0)


def exchange(x, axis):
    return lax.all_to_all(x, axis, 0, 0)


def body(
    tokens,
    attn_gain,
    w_query,
    w_keyval,
    cache,
    lengths,
    write_pos,
    w_out,
    mlp_gain,
    w_gate_up,
    w_down,
):
    n_req = lax.axis_size("req")
    n_ch = lax.axis_size("ch")
    rows = tokens.shape[0]
    feat = tokens.shape[1]
    chan = cache.shape[2]
    window = cache.shape[3]
    total_rows = rows * n_req
    per_ch = n_req // n_ch
    factor = 1.0 / math.sqrt(HD)

    tok_all = gather_rows(tokens, "req", n_req).reshape(total_rows, feat)
    wide = tok_all.astype(jnp.float32)
    squares = jnp.sum(wide * wide, axis=1)
    scaled = (wide * attn_gain[None, :]).astype(jnp.bfloat16)
    joined = jnp.concatenate([w_query, w_keyval], axis=1)
    qcols = w_query.shape[1]
    kcols = w_keyval.shape[1]
    parts = jnp.dot(scaled, joined, preferred_element_type=jnp.float32)
    parts = jnp.concatenate([parts, squares[:, None]], axis=1)
    width = parts.shape[1]
    parts = exchange(parts.reshape(n_req, rows, width), "req")
    parts = exchange(parts.reshape(n_ch, per_ch, rows, width), "ch")
    summed = jnp.sum(parts, axis=0)
    scale = lax.rsqrt(summed[0, :, width - 1] / D + EPSILON)
    q_sum = summed[:, :, :qcols].transpose(1, 0, 2).reshape(rows, H, chan)
    kv_sum = summed[:, :, qcols:qcols + kcols].transpose(1, 0, 2).reshape(rows, 2 * chan)
    queries = (q_sum * scale[:, None, None]).astype(jnp.bfloat16)
    keyval_new = (kv_sum * scale[:, None]).astype(jnp.bfloat16)
    key_new = keyval_new[:, :chan]
    value_new = keyval_new[:, chan:]

    keys = cache[0]
    values_cache = cache[1]
    own_part = jnp.sum(
        queries.astype(jnp.float32) * key_new.astype(jnp.float32)[:, None, :], axis=-1
    )
    score_part = jnp.einsum("bhe,bew->bhw", queries, keys, preferred_element_type=jnp.float32)
    both = jnp.concatenate([score_part, own_part[..., None]], axis=-1)
    hg = H // n_ch
    both = both.reshape(rows, n_ch, hg, window + 1).transpose(1, 0, 2, 3)
    full = jnp.sum(exchange(both, "ch"), axis=0)
    scores = full[..., :window] * factor
    own_score = full[..., window] * factor
    slot_index = jnp.arange(window, dtype=jnp.int32)
    offset = (write_pos[:, None] - 1 - slot_index[None, :]) % window
    usable = offset < lengths[:, None]
    scores = jnp.where(usable[:, None, :], scores, -jnp.inf)
    top = jnp.maximum(jnp.max(scores, axis=-1), own_score)
    weights = jnp.exp(scores - top[..., None])
    own_weight = jnp.exp(own_score - top)
    total = jnp.sum(weights, axis=-1) + own_weight
    packed = jnp.concatenate([weights, own_weight[..., None], total[..., None]], axis=-1)
    back = gather_rows(packed, "ch", n_ch)
    back = back.transpose(1, 0, 2, 3).reshape(rows, H, window + 2)
    weights_low = back[..., :window].astype(jnp.bfloat16)
    own_w = back[..., window]
    tot = back[..., window + 1]
    numer = jnp.einsum(
        "bhw,bew->bhe", weights_low, values_cache, preferred_element_type=jnp.float32
    )
    numer = (
        numer
        + own_w.astype(jnp.bfloat16).astype(jnp.float32)[..., None]
        * value_new.astype(jnp.float32)[:, None, :]
    )
    attn_local = (numer / tot[..., None]).astype(jnp.bfloat16).reshape(rows, H * chan)

    attn_all = gather_rows(attn_local, "req", n_req).reshape(total_rows, H * chan)
    out_parts = jnp.dot(attn_all, w_out, preferred_element_type=jnp.float32)
    ocols = w_out.shape[1]
    out_parts = exchange(out_parts.reshape(n_req, rows, ocols), "req")
    out_parts = exchange(out_parts.reshape(n_ch, per_ch, rows, ocols), "ch")
    out_sum = jnp.sum(out_parts, axis=0).transpose(1, 0, 2).reshape(rows, per_ch * ocols)
    first = (tokens.astype(jnp.float32) + out_sum).astype(jnp.bfloat16)

    first_all = gather_rows(first, "req", n_req).reshape(total_rows, feat)
    wide2 = first_all.astype(jnp.float32)
    squares2 = jnp.sum(wide2 * wide2, axis=1)
    scaled2 = (wide2 * mlp_gain[None, :]).astype(jnp.bfloat16)
    ffn = jnp.dot(scaled2, w_gate_up, preferred_element_type=jnp.float32)
    ffn = jnp.concatenate([ffn, squares2[:, None]], axis=1)
    fw = ffn.shape[1]
    tg = total_rows // n_ch
    ffn = jnp.sum(exchange(ffn.reshape(n_ch, tg, fw), "ch"), axis=0)
    scale2 = lax.rsqrt(ffn[:, fw - 1] / D + EPSILON)
    hidden_cols = w_gate_up.shape[1] // 2
    gate = ffn[:, :hidden_cols] * scale2[:, None]
    up = ffn[:, hidden_cols:2 * hidden_cols] * scale2[:, None]
    hidden = (jax.nn.gelu(gate, approximate=True) * up).astype(jnp.bfloat16)
    hidden_all = gather_rows(hidden, "ch", n_ch).reshape(total_rows, hidden_cols)
    down = jnp.dot(hidden_all, w_down, preferred_element_type=jnp.float32)
    down = jnp.sum(exchange(down.reshape(n_req, rows, down.shape[1]), "req"), axis=0)
    layer_out = (first.astype(jnp.float32) + down).astype(jnp.bfloat16)
    return (layer_out, keyval_new)


def solution(mesh):
    placed = (
        P("req", "ch"),
        P("ch"),
        P("ch", "req"),
        P("ch", "req"),
        P(None, "req", "ch", None),
        P("req"),
        P("req"),
        P("ch", "req"),
        P("ch"),
        P("ch", "req"),
        P("req", "ch"),
    )
    return jax.shard_map(
        body,
        mesh=mesh,
        in_specs=placed,
        out_specs=(P("req", "ch"), P("req", "ch")),
        check_vma=False,
    )
```

time: 729 us -> 192 us (0.26)
  waiting for transfers between devices: 446 us -> 9.13 us
  blocking collectives: 231 us -> 164 us
  between operations: 15 us -> 0.96 us
    unnamed x10 -> x0, waiting for transfers between devices: 295 us -> none
    all_gather x3 -> x0, blocking collectives: 177 us -> none  [the longest x1 60.2 us: body(): lax.all_gather(normed, 'req', axis=0, tiled=True)]
    all_to_all x1 -> x11, blocking collectives: 16.1 us -> 164 us  [the longest x6 84.1 us: exchange(): return lax.all_to_all(x, axis, 0, 0)]
    psum x2 -> x0, waiting for transfers between devices: 134 us -> none  [the longest x1 69.2 us: body(): ffn_total = lax.psum(ffn_parts, 'ch')]
    psum x3 -> x0, blocking collectives: 38.6 us -> none  [the longest x2 26.7 us: rms_norm(): summed = lax.psum(squares, 'ch')]
    unnamed x31 -> x29, local copies, waits for them, and re-layouts: 10.8 us -> 3.04 us
    all_to_all x2 -> x1, waiting for transfers between devices: 16.4 us -> 9.13 us  [exchange(): return lax.all_to_all(x, axis, 0, 0)]
  transfers between devices with their start and end apart: 8 -> 1, of which waited for: 8 -> 1; matrix products, arithmetic and copies ran while one was open for 1% -> 0% of each run, Pallas kernels for 0% -> 0%
where the time goes in v1:
time: 192 us; the launch traced here: 191 us
  blocking collectives  164 us (85%)
  waiting for transfers between devices  9.13 us (5%)
  local copies, waits for them, and re-layouts  6.93 us (4%)
  other arithmetic  4.9 us (3%)
  starting transfers between devices  3.55 us (2%)
    all_to_all x6, blocking collectives, exchange(): return lax.all_to_all(x, axis, 0, 0)  84.1 us
    all_to_all x5, blocking collectives, gather_rows(): return lax.all_to_all(jnp.broadcast_to(x[None], (n,) + x.shape), axis, 0, 0)  80.1 us
    all_to_all x1, waiting for transfers between devices, exchange(): return lax.all_to_all(x, axis, 0, 0)  9.13 us
  transfers between devices with their start and end apart: 1, of which 1 were waited for; matrix products, arithmetic and copies ran while one was open for 0% of the time, Pallas kernels for 0%

profile of v1, /device:TPU:1, one launch (start us, length us, event | category | flops | bytes accessed | tf_op | source)
XLA Modules:
  0.0 190.9 jit_solution(8518202709658176243)
XLA Ops:
  0.6 0.8 broadcast_in_dim.25
  1.5 25.0 %all_to_all.60 = bf16[64,2,512]{2,1,0:T(2,128)(2,1)S(1)} all-to-all(bf16[64,2,512]{2,1,0:T(2,128)(2,1)S(1)} %broadcast_in_dim.25), channel_id=1, replica_groups=mesh['req'=64,'ch'=8] {'req'}, dimensions={0} | all-to-all | bytes 262144 | tf_op jit(solution)/shard_map/all_to_all | solution.py:17
  26.4 0.1 fusion.5
  26.6 0.5 copy.76
  27.2 0.2 copy-done.8
  27.4 0.2 fusion.13
  27.7 14.4 %all_to_all.61 = f32[64,2,73]{2,1,0:T(2,128)S(1)} all-to-all(f32[64,2,73]{2,1,0:T(2,128)S(1)} %copy.77), channel_id=1, replica_groups=mesh['req'=64,'ch'=8] {'req'}, dimensions={0} | all-to-all | bytes 74752 | tf_op jit(solution)/shard_map/all_to_all | solution.py:21
  42.1 13.8 %all_to_all.62 = f32[8,8,2,73]{3,1,2,0:T(8,128)S(1)} all-to-all(f32[8,8,2,73]{3,1,2,0:T(8,128)S(1)} %copy.78), channel_id=1, replica_groups=mesh['req'=64,'ch'=8] {'ch'}, dimensions={0} | all-to-all | bytes 74752 | tf_op jit(solution)/shard_map/all_to_all | solution.py:21
  56.1 0.2 fusion.43
  56.5 0.4 copy-done.5
  57.0 0.2 multiply_reduce_fusion.1
  57.2 0.2 copy.80
  57.4 0.2 fusion.7
  57.7 0.1 concatenate.29
  57.8 0.8 maximum_bitcast_fusion
  58.7 3.5 %all-to-all-start.3 = ((f32[8,2,2,2049]{3,2,1,0:T(2,128)}), f32[8,2,2,2049]{3,2,1,0:T(2,128)S(1)}, u32[]{:S(2)}, u32[]{:S(2)}) async-start(f32[8,2,2,2049]{3,2,1,0:T(2,128)} %maximum_bitcast_fusion), calls=%async_computation.3 | async-start | bytes 557056 | tf_op jit(solution)/shard_map/all_to_all | solution.py:21
  62.3 0.6 copy-done.7
  62.9 0.1 fusion.36
  63.0 9.1 %all-to-all-done.3 = f32[8,2,2,2049]{3,2,1,0:T(2,128)S(1)} async-done(((f32[8,2,2,2049]{3,2,1,0:T(2,128)}), f32[8,2,2,2049]{3,2,1,0:T(2,128)S(1)}, u32[]{:S(2)}, u32[]{:S(2)}) %all-to-all-start.3) | async-done | bytes 262304 | tf_op jit(solution)/shard_map/all_to_all | solution.py:21
  72.2 0.1 fusion.40
  72.3 0.1 copy.82
  72.5 0.2 fusion.46
  72.7 0.1 copy.83
  73.0 12.5 %all_to_all.63 = f32[8,2,2,2050]{3,2,1,0:T(2,128)S(1)} all-to-all(f32[8,2,2,2050]{3,2,1,0:T(2,128)S(1)} %broadcast_in_dim.27), channel_id=1, replica_groups=mesh['req'=64,'ch'=8] {'ch'}, dimensions={0} | all-to-all | bytes 524800 | tf_op jit(solution)/shard_map/all_to_all | solution.py:17
  85.5 0.2 reshape.137
  85.8 0.1 slice_reduce_fusion
  85.9 0.2 fusion.1
  86.3 17.7 %all_to_all.64 = bf16[64,2,512]{2,1,0:T(2,128)(2,1)S(1)} all-to-all(bf16[64,2,512]{2,1,0:T(2,128)(2,1)S(1)} %broadcast_in_dim.29), channel_id=1, replica_groups=mesh['req'=64,'ch'=8] {'req'}, dimensions={0} | all-to-all | bytes 262144 | tf_op jit(solution)/shard_map/all_to_all | solution.py:17
  104.0 0.2 fusion.16
  104.2 0.1 reshape.151
  104.3 14.0 %all_to_all.65 = f32[64,1,128]{2,1,0:T(1,128)S(1)} all-to-all(f32[64,1,128]{2,1,0:T(1,128)S(1)} %reshape.151), channel_id=1, replica_groups=mesh['req'=64,'ch'=8] {'req'}, dimensions={0} | all-to-all | bytes 65536 | tf_op jit(solution)/shard_map/all_to_all | solution.py:21
  118.3 0.5 broadcast.127
  118.8 0.7 reduce.12
  119.8 9.3 %all_to_all.66 = f32[8,1,1024]{2,1,0:T(1,128)S(1)} all-to-all(f32[8,1,1024]{2,1,0:T(1,128)S(1)} %reshape.153), channel_id=1, replica_groups=mesh['req'=64,'ch'=8] {'ch'}, dimensions={0} | all-to-all | bytes 65536 | tf_op jit(solution)/shard_map/all_to_all | solution.py:21
  129.1 0.7 reduce.13
  130.0 0.6 copy-done.4
  130.7 15.4 %all_to_all.67 = bf16[64,2,512]{2,1,0:T(2,128)(2,1)S(1)} all-to-all(bf16[64,2,512]{2,1,0:T(2,128)(2,1)S(1)} %broadcast_in_dim.30), channel_id=1, replica_groups=mesh['req'=64,'ch'=8] {'req'}, dimensions={0} | all-to-all | bytes 262144 | tf_op jit(solution)/shard_map/all_to_all | solution.py:17
  146.1 0.2 multiply_reduce_fusion
  146.4 0.6 copy-done.6
  147.1 0.2 fusion.2
  147.3 14.7 %all_to_all.68 = f32[8,16,385]{2,1,0:T(8,128)S(1)} all-to-all(f32[8,16,385]{2,1,0:T(8,128)S(1)} %pad_maximum_fusion), channel_id=1, replica_groups=mesh['req'=64,'ch'=8] {'ch'}, dimensions={0} | all-to-all | bytes 394240 | tf_op jit(solution)/shard_map/all_to_all | solution.py:21
  162.1 0.1 fusion.39
  162.3 9.6 %all_to_all.69 = bf16[8,16,192]{2,1,0:T(8,128)(2,1)S(1)} all-to-all(bf16[8,16,192]{2,1,0:T(8,128)(2,1)S(1)} %broadcast_in_dim.31), channel_id=1, replica_groups=mesh['req'=64,'ch'=8] {'ch'}, dimensions={0} | all-to-all | bytes 98304 | tf_op jit(solution)/shard_map/all_to_all | solution.py:17
  171.9 0.2 fusion.11
  172.1 0.2 copy.90
  172.3 17.8 %all_to_all.70 = f32[64,2,512]{2,1,0:T(2,128)S(1)} all-to-all(f32[64,2,512]{2,1,0:T(2,128)S(1)} %copy.90), channel_id=1, replica_groups=mesh['req'=64,'ch'=8] {'req'}, dimensions={0} | all-to-all | bytes 524288 | tf_op jit(solution)/shard_map/all_to_all | solution.py:21
  190.2 0.1 reduce_sum.92
  190.3 0.6 add_convert_fusion
  (57 shorter events, 2.1 us)
Async XLA Ops:
  0.6 145.8 %copy-start = (bf16[512,384]{1,0:T(8,128)(2,1)S(1)}, bf16[512,384]{1,0:T(8,128)(2,1)}, u32[]{:S(2)}) copy-start(bf16[512,384]{1,0:T(8,128)(2,1)} %param.20) | copy-start | bytes 1179652
  26.5 0.8 copy-start.8
  26.6 0.7 copy-start.9
  26.6 0.7 copy-start.10
  27.5 29.9 %copy-start.2 = (bf16[2,2,32,2048]{3,2,1,0:T(8,128)(2,1)S(1)}, bf16[2,2,32,2048]{3,2,1,0:T(8,128)(2,1)}, u32[]{:S(2)}) copy-start(bf16[2,2,32,2048]{3,2,1,0:T(8,128)(2,1)} %param.15) | copy-start | bytes 1572868
  56.4 0.5 copy-start.5
  58.7 3.6 %copy-start.11 = (s32[2]{0:T(128)S(1)}, s32[2]{0:T(128)}, u32[]{:S(2)}) copy-start(s32[2]{0:T(128)} %param.17) | copy-start | bytes 28
  58.7 13.5 %all-to-all-start.3 = ((f32[8,2,2,2049]{3,2,1,0:T(2,128)}), f32[8,2,2,2049]{3,2,1,0:T(2,128)S(1)}, u32[]{:S(2)}, u32[]{:S(2)}) async-start(f32[8,2,2,2049]{3,2,1,0:T(2,128)} %maximum_bitcast_fusion), calls=%async_computation.3 | async-start | bytes 557056 | tf_op jit(solution)/shard_map/all_to_all | solution.py:21
  62.2 0.7 copy-start.7
  86.3 17.7 %copy-start.3 = (bf16[512,64]{0,1:T(8,128)(2,1)S(1)}, bf16[512,64]{0,1:T(8,128)(2,1)}, u32[]{:S(2)}) copy-start(bf16[512,64]{0,1:T(8,128)(2,1)} %param.18) | copy-start | bytes 196612
  129.9 0.7 copy-start.4
  146.4 0.7 copy-start.6
  162.0 9.9 %copy-start.1 = (bf16[192,512]{1,0:T(8,128)(2,1)S(1)}, bf16[192,512]{1,0:T(8,128)(2,1)}, u32[]{:S(2)}) copy-start(bf16[192,512]{1,0:T(8,128)(2,1)} %param.21) | copy-start | bytes 589828

commit v2 on v1

--- a/solution.py
+++ b/solution.py
@@ -85,18 +85,28 @@
     weights = jnp.exp(scores - top[..., None])
     own_weight = jnp.exp(own_score - top)
     total = jnp.sum(weights, axis=-1) + own_weight
-    packed = jnp.concatenate([weights, own_weight[..., None], total[..., None]], axis=-1)
+    total_hi = total.astype(jnp.bfloat16)
+    total_lo = (total - total_hi.astype(jnp.float32)).astype(jnp.bfloat16)
+    packed = jnp.concatenate(
+        [
+            weights.astype(jnp.bfloat16),
+            own_weight.astype(jnp.bfloat16)[..., None],
+            total_hi[..., None],
+            total_lo[..., None],
+        ],
+        axis=-1,
+    )
     back = gather_rows(packed, "ch", n_ch)
-    back = back.transpose(1, 0, 2, 3).reshape(rows, H, window + 2)
-    weights_low = back[..., :window].astype(jnp.bfloat16)
-    own_w = back[..., window]
-    tot = back[..., window + 1]
+    back = back.transpose(1, 0, 2, 3).reshape(rows, H, window + 3)
+    weights_low = back[..., :window]
+    own_w = back[..., window].astype(jnp.float32)
+    tot = back[..., window + 1].astype(jnp.float32) + back[..., window + 2].astype(jnp.float32)
     numer = jnp.einsum(
         "bhw,bew->bhe", weights_low, values_cache, preferred_element_type=jnp.float32
     )
     numer = (
         numer
-        + own_w.astype(jnp.bfloat16).astype(jnp.float32)[..., None]
+        + own_w[..., None]
         * value_new.astype(jnp.float32)[:, None, :]
     )
     attn_local = (numer / tot[..., None]).astype(jnp.bfloat16).reshape(rows, H * chan)

time: 192 us -> 190 us (0.990)
  no operation moved by 1% of the time
where the time goes in v2:
time: 190 us; the launch traced here: 189 us
  blocking collectives  163 us (86%)
  waiting for transfers between devices  9.13 us (5%)
  local copies, waits for them, and re-layouts  7.16 us (4%)
  other arithmetic  4.8 us (3%)
  starting transfers between devices  3.55 us (2%)
    all_to_all x6, blocking collectives, exchange(): return lax.all_to_all(x, axis, 0, 0)  84.1 us
    all_to_all x5, blocking collectives, gather_rows(): return lax.all_to_all(jnp.broadcast_to(x[None], (n,) + x.shape), axis, 0, 0)  78.6 us
    all_to_all x1, waiting for transfers between devices, exchange(): return lax.all_to_all(x, axis, 0, 0)  9.13 us
  transfers between devices with their start and end apart: 1, of which 1 were waited for; matrix products, arithmetic and copies ran while one was open for 0% of the time, Pallas kernels for 0%

profile of v2, /device:TPU:1, one launch (start us, length us, event | category | flops | bytes accessed | tf_op | source)
XLA Modules:
  0.0 189.5 jit_solution(11839967091632966667)
XLA Ops:
  0.6 0.8 broadcast_in_dim.25
  1.5 25.0 %all_to_all.60 = bf16[64,2,512]{2,1,0:T(2,128)(2,1)S(1)} all-to-all(bf16[64,2,512]{2,1,0:T(2,128)(2,1)S(1)} %broadcast_in_dim.25), channel_id=1, replica_groups=mesh['req'=64,'ch'=8] {'req'}, dimensions={0} | all-to-all | bytes 262144 | tf_op jit(solution)/shard_map/all_to_all | solution.py:17
  26.4 0.1 fusion.5
  26.6 0.5 copy.76
  27.2 0.2 copy-done.8
  27.4 0.2 fusion.13
  27.7 14.4 %all_to_all.61 = f32[64,2,73]{2,1,0:T(2,128)S(1)} all-to-all(f32[64,2,73]{2,1,0:T(2,128)S(1)} %copy.77), channel_id=1, replica_groups=mesh['req'=64,'ch'=8] {'req'}, dimensions={0} | all-to-all | bytes 74752 | tf_op jit(solution)/shard_map/all_to_all | solution.py:21
  42.1 13.8 %all_to_all.62 = f32[8,8,2,73]{3,1,2,0:T(8,128)S(1)} all-to-all(f32[8,8,2,73]{3,1,2,0:T(8,128)S(1)} %copy.78), channel_id=1, replica_groups=mesh['req'=64,'ch'=8] {'ch'}, dimensions={0} | all-to-all | bytes 74752 | tf_op jit(solution)/shard_map/all_to_all | solution.py:21
  56.1 0.2 fusion.44
  56.5 0.4 copy-done.5
  57.0 0.2 multiply_reduce_fusion.1
  57.2 0.2 copy.80
  57.4 0.2 fusion.7
  57.7 0.1 concatenate.29
  57.8 0.8 maximum_bitcast_fusion
  58.7 3.5 %all-to-all-start.3 = ((f32[8,2,2,2049]{3,2,1,0:T(2,128)}), f32[8,2,2,2049]{3,2,1,0:T(2,128)S(1)}, u32[]{:S(2)}, u32[]{:S(2)}) async-start(f32[8,2,2,2049]{3,2,1,0:T(2,128)} %maximum_bitcast_fusion), calls=%async_computation.3 | async-start | bytes 557056 | tf_op jit(solution)/shard_map/all_to_all | solution.py:21
  62.3 0.6 copy-done.7
  62.9 0.1 fusion.38
  63.0 9.1 %all-to-all-done.3 = f32[8,2,2,2049]{3,2,1,0:T(2,128)S(1)} async-done(((f32[8,2,2,2049]{3,2,1,0:T(2,128)}), f32[8,2,2,2049]{3,2,1,0:T(2,128)S(1)}, u32[]{:S(2)}, u32[]{:S(2)}) %all-to-all-start.3) | async-done | bytes 262304 | tf_op jit(solution)/shard_map/all_to_all | solution.py:21
  72.2 0.1 fusion.49
  72.5 0.2 fusion.26
  72.7 0.1 copy.83
  72.8 0.1 copy.84
  72.9 0.1 copy.85
  73.2 11.1 %all_to_all.63 = bf16[8,2,2,2051]{3,2,1,0:T(2,128)(2,1)S(1)} all-to-all(bf16[8,2,2,2051]{3,2,1,0:T(2,128)(2,1)S(1)} %broadcast_in_dim.27), channel_id=1, replica_groups=mesh['req'=64,'ch'=8] {'ch'}, dimensions={0} | all-to-all | bytes 262528 | tf_op jit(solution)/shard_map/all_to_all | solution.py:17
  84.5 0.1 convert_reduce_fusion
  84.6 0.2 fusion.1
  85.0 17.5 %all_to_all.64 = bf16[64,2,512]{2,1,0:T(2,128)(2,1)S(1)} all-to-all(bf16[64,2,512]{2,1,0:T(2,128)(2,1)S(1)} %broadcast_in_dim.29), channel_id=1, replica_groups=mesh['req'=64,'ch'=8] {'req'}, dimensions={0} | all-to-all | bytes 262144 | tf_op jit(solution)/shard_map/all_to_all | solution.py:17
  102.6 0.2 fusion.16
  102.8 0.1 reshape.152
  102.9 14.0 %all_to_all.65 = f32[64,1,128]{2,1,0:T(1,128)S(1)} all-to-all(f32[64,1,128]{2,1,0:T(1,128)S(1)} %reshape.152), channel_id=1, replica_groups=mesh['req'=64,'ch'=8] {'req'}, dimensions={0} | all-to-all | bytes 65536 | tf_op jit(solution)/shard_map/all_to_all | solution.py:21
  116.9 0.5 broadcast.132
  117.4 0.7 reduce.10
  118.4 9.3 %all_to_all.66 = f32[8,1,1024]{2,1,0:T(1,128)S(1)} all-to-all(f32[8,1,1024]{2,1,0:T(1,128)S(1)} %reshape.154), channel_id=1, replica_groups=mesh['req'=64,'ch'=8] {'ch'}, dimensions={0} | all-to-all | bytes 65536 | tf_op jit(solution)/shard_map/all_to_all | solution.py:21
  127.7 0.7 reduce.11
  128.6 0.6 copy-done.4
  129.3 15.4 %all_to_all.67 = bf16[64,2,512]{2,1,0:T(2,128)(2,1)S(1)} all-to-all(bf16[64,2,512]{2,1,0:T(2,128)(2,1)S(1)} %broadcast_in_dim.30), channel_id=1, replica_groups=mesh['req'=64,'ch'=8] {'req'}, dimensions={0} | all-to-all | bytes 262144 | tf_op jit(solution)/shard_map/all_to_all | solution.py:17
  144.7 0.2 multiply_reduce_fusion
  145.1 0.6 copy-done.6
  145.7 0.2 fusion.2
  145.9 14.7 %all_to_all.68 = f32[8,16,385]{2,1,0:T(8,128)S(1)} all-to-all(f32[8,16,385]{2,1,0:T(8,128)S(1)} %pad_maximum_fusion), channel_id=1, replica_groups=mesh['req'=64,'ch'=8] {'ch'}, dimensions={0} | all-to-all | bytes 394240 | tf_op jit(solution)/shard_map/all_to_all | solution.py:21
  160.7 0.1 fusion.41
  160.9 9.6 %all_to_all.69 = bf16[8,16,192]{2,1,0:T(8,128)(2,1)S(1)} all-to-all(bf16[8,16,192]{2,1,0:T(8,128)(2,1)S(1)} %broadcast_in_dim.31), channel_id=1, replica_groups=mesh['req'=64,'ch'=8] {'ch'}, dimensions={0} | all-to-all | bytes 98304 | tf_op jit(solution)/shard_map/all_to_all | solution.py:17
  170.6 0.2 fusion.11
  170.7 0.2 copy.92
  171.0 17.8 %all_to_all.70 = f32[64,2,512]{2,1,0:T(2,128)S(1)} all-to-all(f32[64,2,512]{2,1,0:T(2,128)S(1)} %copy.92), channel_id=1, replica_groups=mesh['req'=64,'ch'=8] {'req'}, dimensions={0} | all-to-all | bytes 524288 | tf_op jit(solution)/shard_map/all_to_all | solution.py:21
  188.8 0.1 reduce_sum.92
  188.9 0.6 add_convert_fusion
  (59 shorter events, 2.3 us)
Async XLA Ops:
  0.6 144.4 %copy-start = (bf16[512,384]{1,0:T(8,128)(2,1)S(1)}, bf16[512,384]{1,0:T(8,128)(2,1)}, u32[]{:S(2)}) copy-start(bf16[512,384]{1,0:T(8,128)(2,1)} %param.20) | copy-start | bytes 1179652
  26.5 0.8 copy-start.8
  26.6 0.7 copy-start.9
  26.6 0.7 copy-start.10
  27.5 29.9 %copy-start.2 = (bf16[2,2,32,2048]{3,2,1,0:T(8,128)(2,1)S(1)}, bf16[2,2,32,2048]{3,2,1,0:T(8,128)(2,1)}, u32[]{:S(2)}) copy-start(bf16[2,2,32,2048]{3,2,1,0:T(8,128)(2,1)} %param.15) | copy-start | bytes 1572868
  56.4 0.5 copy-start.5
  58.7 3.6 %copy-start.11 = (s32[2]{0:T(128)S(1)}, s32[2]{0:T(128)}, u32[]{:S(2)}) copy-start(s32[2]{0:T(128)} %param.17) | copy-start | bytes 28
  58.7 13.5 %all-to-all-start.3 = ((f32[8,2,2,2049]{3,2,1,0:T(2,128)}), f32[8,2,2,2049]{3,2,1,0:T(2,128)S(1)}, u32[]{:S(2)}, u32[]{:S(2)}) async-start(f32[8,2,2,2049]{3,2,1,0:T(2,128)} %maximum_bitcast_fusion), calls=%async_computation.3 | async-start | bytes 557056 | tf_op jit(solution)/shard_map/all_to_all | solution.py:21
  62.2 0.7 copy-start.7
  85.0 17.6 %copy-start.3 = (bf16[512,64]{0,1:T(8,128)(2,1)S(1)}, bf16[512,64]{0,1:T(8,128)(2,1)}, u32[]{:S(2)}) copy-start(bf16[512,64]{0,1:T(8,128)(2,1)} %param.18) | copy-start | bytes 196612
  128.5 0.7 copy-start.4
  145.0 0.7 copy-start.6
  160.7 9.9 %copy-start.1 = (bf16[192,512]{1,0:T(8,128)(2,1)S(1)}, bf16[192,512]{1,0:T(8,128)(2,1)}, u32[]{:S(2)}) copy-start(bf16[192,512]{1,0:T(8,128)(2,1)} %param.21) | copy-start | bytes 589828

commit v3 on v2

v3 whole, which is shorter than its diff:
```python
import math

import jax
import jax.numpy as jnp
from jax import lax
from jax.sharding import PartitionSpec as P

D = 4096
H = 16
HD = 256


EPSILON = 1e-06


def gather_rows(x, axis, n):
    return lax.all_to_all(jnp.broadcast_to(x[None], (n,) + x.shape), axis, 0, 0)


def exchange(x, axis):
    return lax.all_to_all(x, axis, 0, 0)


def lane_pad(x, lanes=128):
    extra = (-x.shape[-1]) % lanes
    if extra == 0:
        return x
    return jnp.pad(x, [(0, 0)] * (x.ndim - 1) + [(0, extra)])


def body(
    tokens,
    attn_gain,
    w_query,
    w_keyval,
    cache,
    lengths,
    write_pos,
    w_out,
    mlp_gain,
    w_gate_up,
    w_down,
):
    n_req = lax.axis_size("req")
    n_ch = lax.axis_size("ch")
    rows = tokens.shape[0]
    feat = tokens.shape[1]
    chan = cache.shape[2]
    window = cache.shape[3]
    total_rows = rows * n_req
    per_ch = n_req // n_ch
    factor = 1.0 / math.sqrt(HD)

    tok_all = gather_rows(tokens.reshape(rows * feat), "req", n_req).reshape(total_rows, feat)
    wide = tok_all.astype(jnp.float32)
    squares = jnp.sum(wide * wide, axis=1)
    scaled = (wide * attn_gain[None, :]).astype(jnp.bfloat16)
    joined = jnp.concatenate([w_query, w_keyval], axis=1)
    qcols = w_query.shape[1]
    kcols = w_keyval.shape[1]
    parts = jnp.dot(scaled, joined, preferred_element_type=jnp.float32)
    parts = lane_pad(jnp.concatenate([parts, squares[:, None]], axis=1))
    width = parts.shape[1]
    sq_col = qcols + kcols
    parts = exchange(parts.reshape(n_req, rows * width), "req")
    parts = exchange(parts.reshape(n_ch, per_ch * rows * width), "ch")
    summed = jnp.sum(parts, axis=0).reshape(per_ch, rows, width)
    scale = lax.rsqrt(summed[0, :, sq_col] / D + EPSILON)
    q_sum = summed[:, :, :qcols].transpose(1, 0, 2).reshape(rows, H, chan)
    kv_sum = summed[:, :, qcols:qcols + kcols].transpose(1, 0, 2).reshape(rows, 2 * chan)
    queries = (q_sum * scale[:, None, None]).astype(jnp.bfloat16)
    keyval_new = (kv_sum * scale[:, None]).astype(jnp.bfloat16)
    key_new = keyval_new[:, :chan]
    value_new = keyval_new[:, chan:]

    keys = cache[0]
    values_cache = cache[1]
    own_part = jnp.sum(
        queries.astype(jnp.float32) * key_new.astype(jnp.float32)[:, None, :], axis=-1
    )
    score_part = jnp.einsum("bhe,bew->bhw", queries, keys, preferred_element_type=jnp.float32)
    hg = H // n_ch
    score_part = score_part.reshape(rows, n_ch, hg, window).transpose(1, 0, 2, 3)
    own_part = own_part.reshape(rows, n_ch, hg).transpose(1, 0, 2)
    both = jnp.concatenate(
        [score_part.reshape(n_ch, rows * hg * window), lane_pad(own_part.reshape(n_ch, rows * hg))],
        axis=1,
    )
    full = jnp.sum(exchange(both, "ch"), axis=0)
    scores = full[: rows * hg * window].reshape(rows, hg, window) * factor
    own_score = full[rows * hg * window: rows * hg * window + rows * hg].reshape(rows, hg) * factor
    slot_index = jnp.arange(window, dtype=jnp.int32)
    offset = (write_pos[:, None] - 1 - slot_index[None, :]) % window
    usable = offset < lengths[:, None]
    scores = jnp.where(usable[:, None, :], scores, -jnp.inf)
    top = jnp.maximum(jnp.max(scores, axis=-1), own_score)
    weights = jnp.exp(scores - top[..., None])
    own_weight = jnp.exp(own_score - top)
    total = jnp.sum(weights, axis=-1) + own_weight
    total_hi = total.astype(jnp.bfloat16)
    total_lo = (total - total_hi.astype(jnp.float32)).astype(jnp.bfloat16)
    nw = rows * hg * window
    ns = rows * hg
    stats = jnp.stack([own_weight.astype(jnp.bfloat16), total_hi, total_lo], axis=0)
    packed = jnp.concatenate(
        [weights.astype(jnp.bfloat16).reshape(nw), lane_pad(stats.reshape(3 * ns))], axis=0
    )
    back = gather_rows(packed, "ch", n_ch)
    weights_low = back[:, :nw].reshape(n_ch, rows, hg, window).transpose(1, 0, 2, 3)
    weights_low = weights_low.reshape(rows, H, window)
    stats = back[:, nw: nw + 3 * ns].astype(jnp.float32).reshape(n_ch, 3, rows, hg)
    stats = stats.transpose(1, 2, 0, 3).reshape(3, rows, H)
    own_w = stats[0]
    tot = stats[1] + stats[2]
    numer = jnp.einsum(
        "bhw,bew->bhe", weights_low, values_cache, preferred_element_type=jnp.float32
    )
    numer = (
        numer
        + own_w[..., None]
        * value_new.astype(jnp.float32)[:, None, :]
    )
    attn_local = (numer / tot[..., None]).astype(jnp.bfloat16).reshape(rows, H * chan)

    attn_all = gather_rows(attn_local.reshape(rows * H * chan), "req", n_req).reshape(total_rows, H * chan)
    out_parts = jnp.dot(attn_all, w_out, preferred_element_type=jnp.float32)
    ocols = w_out.shape[1]
    out_parts = exchange(out_parts.reshape(n_req, rows * ocols), "req")
    out_parts = exchange(out_parts.reshape(n_ch, per_ch * rows * ocols), "ch")
    out_sum = jnp.sum(out_parts, axis=0).reshape(per_ch, rows, ocols)
    out_sum = out_sum.transpose(1, 0, 2).reshape(rows, per_ch * ocols)
    first = (tokens.astype(jnp.float32) + out_sum).astype(jnp.bfloat16)

    first_all = gather_rows(first.reshape(rows * feat), "req", n_req).reshape(total_rows, feat)
    wide2 = first_all.astype(jnp.float32)
    squares2 = jnp.sum(wide2 * wide2, axis=1)
    scaled2 = (wide2 * mlp_gain[None, :]).astype(jnp.bfloat16)
    ffn = jnp.dot(scaled2, w_gate_up, preferred_element_type=jnp.float32)
    fw = ffn.shape[1]
    tg = total_rows // n_ch
    ffn = jnp.concatenate(
        [ffn.reshape(n_ch, tg * fw), lane_pad(squares2.reshape(n_ch, tg))], axis=1
    )
    ffn = jnp.sum(exchange(ffn, "ch"), axis=0)
    scale2 = lax.rsqrt(ffn[tg * fw: tg * fw + tg] / D + EPSILON)
    ffn = ffn[: tg * fw].reshape(tg, fw)
    hidden_cols = w_gate_up.shape[1] // 2
    gate = ffn[:, :hidden_cols] * scale2[:, None]
    up = ffn[:, hidden_cols:2 * hidden_cols] * scale2[:, None]
    hidden = (jax.nn.gelu(gate, approximate=True) * up).astype(jnp.bfloat16)
    hidden_all = gather_rows(hidden.reshape(tg * hidden_cols), "ch", n_ch).reshape(total_rows, hidden_cols)
    down = jnp.dot(hidden_all, w_down, preferred_element_type=jnp.float32)
    dcols = down.shape[1]
    down = jnp.sum(exchange(down.reshape(n_req, rows * dcols), "req"), axis=0).reshape(rows, dcols)
    layer_out = (first.astype(jnp.float32) + down).astype(jnp.bfloat16)
    return (layer_out, keyval_new)


def solution(mesh):
    placed = (
        P("req", "ch"),
        P("ch"),
        P("ch", "req"),
        P("ch", "req"),
        P(None, "req", "ch", None),
        P("req"),
        P("req"),
        P("ch", "req"),
        P("ch"),
        P("ch", "req"),
        P("req", "ch"),
    )
    return jax.shard_map(
        body,
        mesh=mesh,
        in_specs=placed,
        out_specs=(P("req", "ch"), P("req", "ch")),
        check_vma=False,
    )
```

time: 190 us -> 199 us (1.047)
  other arithmetic: 4.8 us -> 11.4 us
  local copies, waits for them, and re-layouts: 7.16 us -> 11.2 us
  blocking collectives: 163 us -> 161 us
    broadcast_in_dim x0 -> x5, other arithmetic: none -> 6.47 us  [gather_rows(): return lax.all_to_all(jnp.broadcast_to(x[None], (n,) + x.shape), axis, 0, 0)]
    unnamed x30 -> x39, local copies, waits for them, and re-layouts: 3.14 us -> 5.99 us
where the time goes in v3:
time: 199 us; the launch traced here: 198 us
  blocking collectives  161 us (81%)
  other arithmetic  11.4 us (6%)
  local copies, waits for them, and re-layouts  11.2 us (6%)
  waiting for transfers between devices  8.78 us (4%)
  starting transfers between devices  3.54 us (2%)
    all_to_all x6, blocking collectives, exchange(): return lax.all_to_all(x, axis, 0, 0)  82.8 us
    all_to_all x5, blocking collectives, gather_rows(): return lax.all_to_all(jnp.broadcast_to(x[None], (n,) + x.shape), axis, 0, 0)  78.3 us
    all_to_all x1, waiting for transfers between devices, exchange(): return lax.all_to_all(x, axis, 0, 0)  8.78 us
    broadcast_in_dim x5, other arithmetic, gather_rows(): return lax.all_to_all(jnp.broadcast_to(x[None], (n,) + x.shape), axis, 0, 0)  6.47 us
    unnamed x39, local copies, waits for them, and re-layouts  5.99 us
  transfers between devices with their start and end apart: 1, of which 1 were waited for; matrix products, arithmetic and copies ran while one was open for 0% of the time, Pallas kernels for 0%

profile of v3, /device:TPU:1, one launch (start us, length us, event | category | flops | bytes accessed | tf_op | source)
XLA Modules:
  0.0 198.3 jit_solution(12316305216160697969)
XLA Ops:
  0.6 0.7 copy.113
  1.5 0.5 broadcast.171
  2.0 1.4 reduce.13
  3.5 25.0 %all_to_all.97 = bf16[64,2,512]{2,1,0:T(2,128)(2,1)S(1)} all-to-all(bf16[64,2,512]{2,1,0:T(2,128)(2,1)S(1)} %reshape.353), channel_id=1, replica_groups=mesh['req'=64,'ch'=8] {'req'}, dimensions={0} | all-to-all | bytes 262144 | tf_op jit(solution)/shard_map/all_to_all | solution.py:17
  28.6 0.7 convert_reduce_fusion.1
  29.5 0.7 copy-done.3
  30.2 0.2 fusion.8
  30.5 14.4 %all_to_all.98 = f32[64,1,256]{2,1,0:T(1,128)S(1)} all-to-all(f32[64,1,256]{2,1,0:T(1,128)S(1)} %bitcast.73), channel_id=1, replica_groups=mesh['req'=64,'ch'=8] {'req'}, dimensions={0} | all-to-all | bytes 131072 | tf_op jit(solution)/shard_map/all_to_all | solution.py:21
  44.9 13.8 %all_to_all.99 = f32[8,1,2048]{2,1,0:T(1,128)S(1)} all-to-all(f32[8,1,2048]{2,1,0:T(1,128)S(1)} %bitcast.74), channel_id=1, replica_groups=mesh['req'=64,'ch'=8] {'ch'}, dimensions={0} | all-to-all | bytes 131072 | tf_op jit(solution)/shard_map/all_to_all | solution.py:21
  58.9 0.2 fusion.32
  59.3 0.4 copy-done.7
  59.8 0.2 multiply_reduce_fusion.2
  60.3 0.2 fusion.4
  60.7 0.2 reshape.329
  60.9 1.0 copy.100
  61.9 3.5 %all-to-all-start.3 = ((f32[8,1,8320]{2,1,0:T(1,128)}), f32[8,1,8320]{2,1,0:T(1,128)S(1)}, u32[]{:S(2)}, u32[]{:S(2)}) async-start(f32[8,1,8320]{2,1,0:T(1,128)} %copy.100), calls=%async_computation.3 | async-start | bytes 532480 | tf_op jit(solution)/shard_map/all_to_all | solution.py:21
  65.5 0.6 copy-done.10
  66.3 8.8 %all-to-all-done.3 = f32[8,1,8320]{2,1,0:T(1,128)S(1)} async-done(((f32[8,1,8320]{2,1,0:T(1,128)}), f32[8,1,8320]{2,1,0:T(1,128)S(1)}, u32[]{:S(2)}, u32[]{:S(2)}) %all-to-all-start.3) | async-done | bytes 266272 | tf_op jit(solution)/shard_map/all_to_all | solution.py:21
  75.1 0.2 reduce_sum.86
  75.6 0.2 broadcast_bitcast_fusion
  76.1 1.4 reduce.14
  77.7 10.9 %all_to_all.100 = bf16[8,2,4160]{2,1,0:T(2,128)(2,1)S(1)} all-to-all(bf16[8,2,4160]{2,1,0:T(2,128)(2,1)S(1)} %reshape.355), channel_id=1, replica_groups=mesh['req'=64,'ch'=8] {'ch'}, dimensions={0} | all-to-all | bytes 266240 | tf_op jit(solution)/shard_map/all_to_all | solution.py:17
  89.4 0.2 fusion.1
  89.7 0.1 broadcast_in_dim.76
  89.9 1.4 reduce.15
  91.3 17.6 %all_to_all.101 = bf16[64,2,512]{2,1,0:T(2,128)(2,1)S(1)} all-to-all(bf16[64,2,512]{2,1,0:T(2,128)(2,1)S(1)} %reshape.357), channel_id=1, replica_groups=mesh['req'=64,'ch'=8] {'req'}, dimensions={0} | all-to-all | bytes 262144 | tf_op jit(solution)/shard_map/all_to_all | solution.py:17
  109.0 0.7 reduce.7
  109.8 0.8 copy-done.4
  110.6 0.2 fusion.40
  110.8 14.0 %all_to_all.102 = f32[64,1,128]{2,1,0:T(1,128)S(1)} all-to-all(f32[64,1,128]{2,1,0:T(1,128)S(1)} %bitcast.75), channel_id=1, replica_groups=mesh['req'=64,'ch'=8] {'req'}, dimensions={0} | all-to-all | bytes 65536 | tf_op jit(solution)/shard_map/all_to_all | solution.py:21
  124.8 9.3 %all_to_all.103 = f32[8,1,1024]{2,1,0:T(1,128)S(1)} all-to-all(f32[8,1,1024]{2,1,0:T(1,128)S(1)} %bitcast.76), channel_id=1, replica_groups=mesh['req'=64,'ch'=8] {'ch'}, dimensions={0} | all-to-all | bytes 65536 | tf_op jit(solution)/shard_map/all_to_all | solution.py:21
  134.4 0.6 copy-done.5
  135.1 1.4 reduce.16
  136.6 15.4 %all_to_all.104 = bf16[64,2,512]{2,1,0:T(2,128)(2,1)S(1)} all-to-all(bf16[64,2,512]{2,1,0:T(2,128)(2,1)S(1)} %reshape.359), channel_id=1, replica_groups=mesh['req'=64,'ch'=8] {'req'}, dimensions={0} | all-to-all | bytes 262144 | tf_op jit(solution)/shard_map/all_to_all | solution.py:17
  152.1 0.7 convert_reduce_fusion
  153.1 0.6 copy-done.9
  153.7 0.2 fusion.9
  154.1 12.5 %all_to_all.105 = f32[8,1,6272]{2,1,0:T(1,128)S(1)} all-to-all(f32[8,1,6272]{2,1,0:T(1,128)S(1)} %all_to_all.79), channel_id=1, replica_groups=mesh['req'=64,'ch'=8] {'ch'}, dimensions={0} | all-to-all | bytes 401408 | tf_op jit(solution)/shard_map/all_to_all | solution.py:21
  166.6 0.2 reduce_sum.91
  167.0 0.9 reduce.17
  168.0 9.4 %all_to_all.106 = bf16[8,2,1536]{2,1,0:T(2,128)(2,1)S(1)} all-to-all(bf16[8,2,1536]{2,1,0:T(2,128)(2,1)S(1)} %reshape.361), channel_id=1, replica_groups=mesh['req'=64,'ch'=8] {'ch'}, dimensions={0} | all-to-all | bytes 98304 | tf_op jit(solution)/shard_map/all_to_all | solution.py:17
  177.4 0.3 reduce.9
  177.9 0.5 copy-done.1
  178.3 0.2 fusion.41
  178.5 0.3 all_to_all.84
  178.8 18.7 %all_to_all.107 = f32[64,1,1024]{2,1,0:T(1,128)S(1)} all-to-all(f32[64,1,1024]{2,1,0:T(1,128)S(1)} %all_to_all.84), channel_id=1, replica_groups=mesh['req'=64,'ch'=8] {'req'}, dimensions={0} | all-to-all | bytes 524288 | tf_op jit(solution)/shard_map/all_to_all | solution.py:21
  197.6 0.2 reduce_sum.92
  197.7 0.6 add_convert_fusion
  (102 shorter events, 5.0 us)
Async XLA Ops:
  0.6 152.4 %copy-start = (bf16[512,384]{1,0:T(8,128)(2,1)S(1)}, bf16[512,384]{1,0:T(8,128)(2,1)}, u32[]{:S(2)}) copy-start(bf16[512,384]{1,0:T(8,128)(2,1)} %param.20) | copy-start | bytes 1179652
  29.3 0.8 copy-start.3
  29.3 0.8 copy-start.6
  29.4 0.8 copy-start.8
  30.2 30.1 %copy-start.2 = (bf16[2,2,32,2048]{3,2,1,0:T(8,128)(2,1)S(1)}, bf16[2,2,32,2048]{3,2,1,0:T(8,128)(2,1)}, u32[]{:S(2)}) copy-start(bf16[2,2,32,2048]{3,2,1,0:T(8,128)(2,1)} %param.15) | copy-start | bytes 1572868
  59.2 0.5 copy-start.7
  61.9 3.6 %copy-start.11 = (s32[2]{0:T(128)S(1)}, s32[2]{0:T(128)}, u32[]{:S(2)}) copy-start(s32[2]{0:T(128)} %param.17) | copy-start | bytes 28
  61.9 13.2 %all-to-all-start.3 = ((f32[8,1,8320]{2,1,0:T(1,128)}), f32[8,1,8320]{2,1,0:T(1,128)S(1)}, u32[]{:S(2)}, u32[]{:S(2)}) async-start(f32[8,1,8320]{2,1,0:T(1,128)} %copy.100), calls=%async_computation.3 | async-start | bytes 532480 | tf_op jit(solution)/shard_map/all_to_all | solution.py:21
  65.5 0.7 copy-start.10
  109.8 0.8 copy-start.4
  134.3 0.7 copy-start.5
  153.0 0.7 copy-start.9
  177.4 0.9 copy-start.1

commit v4 on v2

--- a/solution.py
+++ b/solution.py
@@ -124,18 +124,22 @@
     squares2 = jnp.sum(wide2 * wide2, axis=1)
     scaled2 = (wide2 * mlp_gain[None, :]).astype(jnp.bfloat16)
     ffn = jnp.dot(scaled2, w_gate_up, preferred_element_type=jnp.float32)
-    ffn = jnp.concatenate([ffn, squares2[:, None]], axis=1)
+    sq_hi = squares2.astype(jnp.bfloat16)
+    sq_lo = (squares2 - sq_hi.astype(jnp.float32)).astype(jnp.bfloat16)
+    ffn = jnp.concatenate([ffn.astype(jnp.bfloat16), sq_hi[:, None], sq_lo[:, None]], axis=1)
     fw = ffn.shape[1]
     tg = total_rows // n_ch
-    ffn = jnp.sum(exchange(ffn.reshape(n_ch, tg, fw), "ch"), axis=0)
-    scale2 = lax.rsqrt(ffn[:, fw - 1] / D + EPSILON)
+    ffn = exchange(ffn.reshape(n_ch, tg, fw), "ch")
+    ffn = jnp.sum(ffn.astype(jnp.float32), axis=0)
+    scale2 = lax.rsqrt((ffn[:, fw - 2] + ffn[:, fw - 1]) / D + EPSILON)
     hidden_cols = w_gate_up.shape[1] // 2
     gate = ffn[:, :hidden_cols] * scale2[:, None]
     up = ffn[:, hidden_cols:2 * hidden_cols] * scale2[:, None]
     hidden = (jax.nn.gelu(gate, approximate=True) * up).astype(jnp.bfloat16)
     hidden_all = gather_rows(hidden, "ch", n_ch).reshape(total_rows, hidden_cols)
     down = jnp.dot(hidden_all, w_down, preferred_element_type=jnp.float32)
-    down = jnp.sum(exchange(down.reshape(n_req, rows, down.shape[1]), "req"), axis=0)
+    down = exchange(down.astype(jnp.bfloat16).reshape(n_req, rows, down.shape[1]), "req")
+    down = jnp.sum(down.astype(jnp.float32), axis=0)
     layer_out = (first.astype(jnp.float32) + down).astype(jnp.bfloat16)
     return (layer_out, keyval_new)
 

time: 190 us -> 186 us (0.979)
  blocking collectives: 163 us -> 158 us
    all_to_all x6, blocking collectives: 84.1 us -> 79.6 us  [exchange(): return lax.all_to_all(x, axis, 0, 0)]
where the time goes in v4:
time: 186 us; the launch traced here: 185 us
  blocking collectives  158 us (85%)
  waiting for transfers between devices  9.13 us (5%)
  local copies, waits for them, and re-layouts  7.25 us (4%)
  other arithmetic  4.98 us (3%)
  starting transfers between devices  3.55 us (2%)
    all_to_all x6, blocking collectives, exchange(): return lax.all_to_all(x, axis, 0, 0)  79.6 us
    all_to_all x5, blocking collectives, gather_rows(): return lax.all_to_all(jnp.broadcast_to(x[None], (n,) + x.shape), axis, 0, 0)  78.7 us
    all_to_all x1, waiting for transfers between devices, exchange(): return lax.all_to_all(x, axis, 0, 0)  9.13 us
  transfers between devices with their start and end apart: 1, of which 1 were waited for; matrix products, arithmetic and copies ran while one was open for 0% of the time, Pallas kernels for 0%

profile of v4, /device:TPU:1, one launch (start us, length us, event | category | flops | bytes accessed | tf_op | source)
XLA Modules:
  0.0 185.3 jit_solution(13525587640339162975)
XLA Ops:
  0.6 0.8 broadcast_in_dim.25
  1.5 25.0 %all_to_all.60 = bf16[64,2,512]{2,1,0:T(2,128)(2,1)S(1)} all-to-all(bf16[64,2,512]{2,1,0:T(2,128)(2,1)S(1)} %broadcast_in_dim.25), channel_id=1, replica_groups=mesh['req'=64,'ch'=8] {'req'}, dimensions={0} | all-to-all | bytes 262144 | tf_op jit(solution)/shard_map/all_to_all | solution.py:17
  26.4 0.1 fusion.3
  26.6 0.5 copy.109
  27.2 0.2 copy-done.8
  27.4 0.2 fusion.9
  27.7 14.4 %all_to_all.61 = f32[64,2,73]{2,1,0:T(2,128)S(1)} all-to-all(f32[64,2,73]{2,1,0:T(2,128)S(1)} %copy.110), channel_id=1, replica_groups=mesh['req'=64,'ch'=8] {'req'}, dimensions={0} | all-to-all | bytes 74752 | tf_op jit(solution)/shard_map/all_to_all | solution.py:21
  42.1 13.8 %all_to_all.62 = f32[8,8,2,73]{3,1,2,0:T(8,128)S(1)} all-to-all(f32[8,8,2,73]{3,1,2,0:T(8,128)S(1)} %copy.111), channel_id=1, replica_groups=mesh['req'=64,'ch'=8] {'ch'}, dimensions={0} | all-to-all | bytes 74752 | tf_op jit(solution)/shard_map/all_to_all | solution.py:21
  56.0 0.2 fusion.40
  56.5 0.4 copy-done.5
  57.0 0.2 multiply_reduce_fusion.1
  57.2 0.2 copy.113
  57.4 0.2 fusion.5
  57.7 0.1 concatenate.29
  57.8 0.8 maximum_bitcast_fusion
  58.7 3.5 %all-to-all-start.3 = ((f32[8,2,2,2049]{3,2,1,0:T(2,128)}), f32[8,2,2,2049]{3,2,1,0:T(2,128)S(1)}, u32[]{:S(2)}, u32[]{:S(2)}) async-start(f32[8,2,2,2049]{3,2,1,0:T(2,128)} %maximum_bitcast_fusion), calls=%async_computation.3 | async-start | bytes 557056 | tf_op jit(solution)/shard_map/all_to_all | solution.py:21
  62.3 0.6 copy-done.7
  63.0 9.1 %all-to-all-done.3 = f32[8,2,2,2049]{3,2,1,0:T(2,128)S(1)} async-done(((f32[8,2,2,2049]{3,2,1,0:T(2,128)}), f32[8,2,2,2049]{3,2,1,0:T(2,128)S(1)}, u32[]{:S(2)}, u32[]{:S(2)}) %all-to-all-start.3) | async-done | bytes 262304 | tf_op jit(solution)/shard_map/all_to_all | solution.py:21
  72.2 0.1 fusion.45
  72.5 0.2 fusion.21
  72.7 0.1 copy.116
  72.8 0.1 copy.117
  72.9 0.1 copy.118
  73.2 11.1 %all_to_all.63 = bf16[8,2,2,2051]{3,2,1,0:T(2,128)(2,1)S(1)} all-to-all(bf16[8,2,2,2051]{3,2,1,0:T(2,128)(2,1)S(1)} %broadcast_in_dim.27), channel_id=1, replica_groups=mesh['req'=64,'ch'=8] {'ch'}, dimensions={0} | all-to-all | bytes 262528 | tf_op jit(solution)/shard_map/all_to_all | solution.py:17
  84.5 0.1 convert_reduce_fusion.2
  84.6 0.2 fusion.1
  85.0 17.5 %all_to_all.64 = bf16[64,2,512]{2,1,0:T(2,128)(2,1)S(1)} all-to-all(bf16[64,2,512]{2,1,0:T(2,128)(2,1)S(1)} %broadcast_in_dim.29), channel_id=1, replica_groups=mesh['req'=64,'ch'=8] {'req'}, dimensions={0} | all-to-all | bytes 262144 | tf_op jit(solution)/shard_map/all_to_all | solution.py:17
  102.6 0.2 fusion.12
  102.8 0.1 reshape.180
  102.9 14.0 %all_to_all.65 = f32[64,1,128]{2,1,0:T(1,128)S(1)} all-to-all(f32[64,1,128]{2,1,0:T(1,128)S(1)} %reshape.180), channel_id=1, replica_groups=mesh['req'=64,'ch'=8] {'req'}, dimensions={0} | all-to-all | bytes 65536 | tf_op jit(solution)/shard_map/all_to_all | solution.py:21
  116.9 0.5 broadcast.127
  117.4 0.7 reduce.10
  118.4 9.3 %all_to_all.66 = f32[8,1,1024]{2,1,0:T(1,128)S(1)} all-to-all(f32[8,1,1024]{2,1,0:T(1,128)S(1)} %reshape.182), channel_id=1, replica_groups=mesh['req'=64,'ch'=8] {'ch'}, dimensions={0} | all-to-all | bytes 65536 | tf_op jit(solution)/shard_map/all_to_all | solution.py:21
  127.7 0.7 reduce.11
  128.6 0.6 copy-done.4
  129.3 15.4 %all_to_all.67 = bf16[64,2,512]{2,1,0:T(2,128)(2,1)S(1)} all-to-all(bf16[64,2,512]{2,1,0:T(2,128)(2,1)S(1)} %broadcast_in_dim.30), channel_id=1, replica_groups=mesh['req'=64,'ch'=8] {'req'}, dimensions={0} | all-to-all | bytes 262144 | tf_op jit(solution)/shard_map/all_to_all | solution.py:17
  144.7 0.2 multiply_reduce_fusion
  145.0 0.1 copy.125
  145.2 0.1 copy.126
  145.3 0.6 copy-done.6
  146.0 0.2 convolution_convert_fusion.1
  146.3 10.7 %all_to_all.68 = bf16[8,16,386]{2,1,0:T(8,128)(2,1)S(1)} all-to-all(bf16[8,16,386]{2,1,0:T(8,128)(2,1)S(1)} %pad_maximum_fusion), channel_id=1, replica_groups=mesh['req'=64,'ch'=8] {'ch'}, dimensions={0} | all-to-all | bytes 197632 | tf_op jit(solution)/shard_map/all_to_all | solution.py:21
  157.0 0.2 fusion.37
  157.3 9.7 %all_to_all.69 = bf16[8,16,192]{2,1,0:T(8,128)(2,1)S(1)} all-to-all(bf16[8,16,192]{2,1,0:T(8,128)(2,1)S(1)} %broadcast_in_dim.31), channel_id=1, replica_groups=mesh['req'=64,'ch'=8] {'ch'}, dimensions={0} | all-to-all | bytes 98304 | tf_op jit(solution)/shard_map/all_to_all | solution.py:17
  167.0 0.2 convolution_convert_fusion
  167.3 17.2 %all_to_all.70 = bf16[64,2,512]{2,1,0:T(2,128)(2,1)S(1)} all-to-all(bf16[64,2,512]{2,1,0:T(2,128)(2,1)S(1)} %reshape.171), channel_id=1, replica_groups=mesh['req'=64,'ch'=8] {'req'}, dimensions={0} | all-to-all | bytes 262144 | tf_op jit(solution)/shard_map/all_to_all | solution.py:21
  184.5 0.1 convert_reduce_fusion
  184.7 0.6 add_convert_fusion
  (61 shorter events, 2.5 us)
Async XLA Ops:
  0.6 144.7 %copy-start = (bf16[512,384]{1,0:T(8,128)(2,1)S(1)}, bf16[512,384]{1,0:T(8,128)(2,1)}, u32[]{:S(2)}) copy-start(bf16[512,384]{1,0:T(8,128)(2,1)} %param.20) | copy-start | bytes 1179652
  26.5 0.8 copy-start.8
  26.6 0.7 copy-start.9
  26.6 0.7 copy-start.10
  27.5 29.9 %copy-start.2 = (bf16[2,2,32,2048]{3,2,1,0:T(8,128)(2,1)S(1)}, bf16[2,2,32,2048]{3,2,1,0:T(8,128)(2,1)}, u32[]{:S(2)}) copy-start(bf16[2,2,32,2048]{3,2,1,0:T(8,128)(2,1)} %param.15) | copy-start | bytes 1572868
  56.4 0.5 copy-start.5
  58.7 3.6 %copy-start.11 = (s32[2]{0:T(128)S(1)}, s32[2]{0:T(128)}, u32[]{:S(2)}) copy-start(s32[2]{0:T(128)} %param.17) | copy-start | bytes 28
  58.7 13.5 %all-to-all-start.3 = ((f32[8,2,2,2049]{3,2,1,0:T(2,128)}), f32[8,2,2,2049]{3,2,1,0:T(2,128)S(1)}, u32[]{:S(2)}, u32[]{:S(2)}) async-start(f32[8,2,2,2049]{3,2,1,0:T(2,128)} %maximum_bitcast_fusion), calls=%async_computation.3 | async-start | bytes 557056 | tf_op jit(solution)/shard_map/all_to_all | solution.py:21
  62.2 0.7 copy-start.7
  85.0 17.6 %copy-start.3 = (bf16[512,64]{0,1:T(8,128)(2,1)S(1)}, bf16[512,64]{0,1:T(8,128)(2,1)}, u32[]{:S(2)}) copy-start(bf16[512,64]{0,1:T(8,128)(2,1)} %param.18) | copy-start | bytes 196612
  128.5 0.7 copy-start.4
  145.3 0.7 copy-start.6
  157.0 10.0 %copy-start.1 = (bf16[192,512]{1,0:T(8,128)(2,1)S(1)}, bf16[192,512]{1,0:T(8,128)(2,1)}, u32[]{:S(2)}) copy-start(bf16[192,512]{1,0:T(8,128)(2,1)} %param.21) | copy-start | bytes 589828

commit v5 on v4

--- a/solution.py
+++ b/solution.py
@@ -112,11 +112,14 @@
     attn_local = (numer / tot[..., None]).astype(jnp.bfloat16).reshape(rows, H * chan)
 
     attn_all = gather_rows(attn_local, "req", n_req).reshape(total_rows, H * chan)
-    out_parts = jnp.dot(attn_all, w_out, preferred_element_type=jnp.float32)
     ocols = w_out.shape[1]
-    out_parts = exchange(out_parts.reshape(n_req, rows, ocols), "req")
-    out_parts = exchange(out_parts.reshape(n_ch, per_ch, rows, ocols), "ch")
-    out_sum = jnp.sum(out_parts, axis=0).transpose(1, 0, 2).reshape(rows, per_ch * ocols)
+    lanes = max(ocols, 128)
+    w_out_wide = jnp.pad(w_out, ((0, 0), (0, lanes - ocols)))
+    out_parts = jnp.dot(attn_all, w_out_wide, preferred_element_type=jnp.float32)
+    out_parts = exchange(out_parts.reshape(n_req, rows, lanes), "req")
+    out_parts = exchange(out_parts.reshape(n_ch, per_ch, rows, lanes), "ch")
+    out_sum = jnp.sum(out_parts, axis=0)[..., :ocols]
+    out_sum = out_sum.transpose(1, 0, 2).reshape(rows, per_ch * ocols)
     first = (tokens.astype(jnp.float32) + out_sum).astype(jnp.bfloat16)
 
     first_all = gather_rows(first, "req", n_req).reshape(total_rows, feat)

time: 186 us -> 186 us (level)
  blocking collectives: 158 us -> 141 us
  waiting for transfers between devices: 9.13 us -> 19.4 us
  starting transfers between devices: 3.55 us -> 11.4 us
    all_to_all x5 -> x4, blocking collectives: 78.7 us -> 61.2 us  [gather_rows(): return lax.all_to_all(jnp.broadcast_to(x[None], (n,) + x.shape), axis, 0, 0)]
    all_to_all x0 -> x1, waiting for transfers between devices: none -> 10.3 us  [gather_rows(): return lax.all_to_all(jnp.broadcast_to(x[None], (n,) + x.shape), axis, 0, 0)]
    all_to_all x0 -> x1, starting transfers between devices: none -> 7.83 us  [gather_rows(): return lax.all_to_all(jnp.broadcast_to(x[None], (n,) + x.shape), axis, 0, 0)]
  transfers between devices with their start and end apart: 1 -> 2, of which waited for: 1 -> 2; matrix products, arithmetic and copies ran while one was open for 0% -> 0% of each run, Pallas kernels for 0% -> 0%
where the time goes in v5:
time: 186 us; the launch traced here: 185 us
  blocking collectives  141 us (76%)
  waiting for transfers between devices  19.4 us (10%)
  starting transfers between devices  11.4 us (6%)
  local copies, waits for them, and re-layouts  7.11 us (4%)
  other arithmetic  3.54 us (2%)
    all_to_all x6, blocking collectives, exchange(): return lax.all_to_all(x, axis, 0, 0)  80.1 us
    all_to_all x4, blocking collectives, gather_rows(): return lax.all_to_all(jnp.broadcast_to(x[None], (n,) + x.shape), axis, 0, 0)  61.2 us
    all_to_all x1, waiting for transfers between devices, gather_rows(): return lax.all_to_all(jnp.broadcast_to(x[None], (n,) + x.shape), axis, 0, 0)  10.3 us
    all_to_all x1, waiting for transfers between devices, exchange(): return lax.all_to_all(x, axis, 0, 0)  9.13 us
    all_to_all x1, starting transfers between devices, gather_rows(): return lax.all_to_all(jnp.broadcast_to(x[None], (n,) + x.shape), axis, 0, 0)  7.83 us
  transfers between devices with their start and end apart: 2, of which 2 were waited for; matrix products, arithmetic and copies ran while one was open for 0% of the time, Pallas kernels for 0%

profile of v5, /device:TPU:1, one launch (start us, length us, event | category | flops | bytes accessed | tf_op | source)
XLA Modules:
  0.0 184.9 jit_solution(6079953975145882686)
XLA Ops:
  0.6 0.8 broadcast_in_dim.25
  1.5 25.0 %all_to_all.60 = bf16[64,2,512]{2,1,0:T(2,128)(2,1)S(1)} all-to-all(bf16[64,2,512]{2,1,0:T(2,128)(2,1)S(1)} %broadcast_in_dim.25), channel_id=1, replica_groups=mesh['req'=64,'ch'=8] {'req'}, dimensions={0} | all-to-all | bytes 262144 | tf_op jit(solution)/shard_map/all_to_all | solution.py:17
  26.4 0.1 fusion.3
  26.6 0.5 copy.116
  27.2 0.2 copy-done.8
  27.4 0.2 fusion.9
  27.7 14.4 %all_to_all.61 = f32[64,2,73]{2,1,0:T(2,128)S(1)} all-to-all(f32[64,2,73]{2,1,0:T(2,128)S(1)} %copy.117), channel_id=1, replica_groups=mesh['req'=64,'ch'=8] {'req'}, dimensions={0} | all-to-all | bytes 74752 | tf_op jit(solution)/shard_map/all_to_all | solution.py:21
  42.1 13.8 %all_to_all.62 = f32[8,8,2,73]{3,1,2,0:T(8,128)S(1)} all-to-all(f32[8,8,2,73]{3,1,2,0:T(8,128)S(1)} %copy.118), channel_id=1, replica_groups=mesh['req'=64,'ch'=8] {'ch'}, dimensions={0} | all-to-all | bytes 74752 | tf_op jit(solution)/shard_map/all_to_all | solution.py:21
  56.0 0.2 fusion.41
  56.5 0.4 copy-done.5
  57.0 0.2 multiply_reduce_fusion.1
  57.2 0.2 copy.120
  57.4 0.2 fusion.5
  57.7 0.1 concatenate.29
  57.8 0.8 maximum_bitcast_fusion
  58.7 3.5 %all-to-all-start.3 = ((f32[8,2,2,2049]{3,2,1,0:T(2,128)}), f32[8,2,2,2049]{3,2,1,0:T(2,128)S(1)}, u32[]{:S(2)}, u32[]{:S(2)}) async-start(f32[8,2,2,2049]{3,2,1,0:T(2,128)} %maximum_bitcast_fusion), calls=%async_computation.3 | async-start | bytes 557056 | tf_op jit(solution)/shard_map/all_to_all | solution.py:21
  62.3 0.6 copy-done.7
  62.9 0.1 fusion.34
  63.0 9.1 %all-to-all-done.3 = f32[8,2,2,2049]{3,2,1,0:T(2,128)S(1)} async-done(((f32[8,2,2,2049]{3,2,1,0:T(2,128)}), f32[8,2,2,2049]{3,2,1,0:T(2,128)S(1)}, u32[]{:S(2)}, u32[]{:S(2)}) %all-to-all-start.3) | async-done | bytes 262304 | tf_op jit(solution)/shard_map/all_to_all | solution.py:21
  72.2 0.1 fusion.47
  72.5 0.2 fusion.22
  72.7 0.1 copy.123
  72.8 0.1 copy.124
  72.9 0.1 copy.125
  73.2 11.1 %all_to_all.63 = bf16[8,2,2,2051]{3,2,1,0:T(2,128)(2,1)S(1)} all-to-all(bf16[8,2,2,2051]{3,2,1,0:T(2,128)(2,1)S(1)} %broadcast_in_dim.27), channel_id=1, replica_groups=mesh['req'=64,'ch'=8] {'ch'}, dimensions={0} | all-to-all | bytes 262528 | tf_op jit(solution)/shard_map/all_to_all | solution.py:17
  84.5 0.1 convert_reduce_fusion.2
  84.6 0.2 fusion.1
  84.9 0.7 broadcast_in_dim.29
  85.7 7.8 %all-to-all-start.5 = ((bf16[64,2,512]{2,1,0:T(2,128)(2,1)}), bf16[64,2,512]{2,1,0:T(2,128)(2,1)S(1)}, u32[]{:S(2)}, u32[]{:S(2)}) async-start(bf16[64,2,512]{2,1,0:T(2,128)(2,1)} %broadcast_in_dim.29), calls=%async_computation.5 | async-start | bytes 262144 | tf_op jit(solution)/shard_map/all_to_all | solution.py:17
  93.5 0.1 copy.127
  93.6 10.3 %all-to-all-done.5 = bf16[64,2,512]{2,1,0:T(2,128)(2,1)S(1)} async-done(((bf16[64,2,512]{2,1,0:T(2,128)(2,1)}), bf16[64,2,512]{2,1,0:T(2,128)(2,1)S(1)}, u32[]{:S(2)}, u32[]{:S(2)}) %all-to-all-start.5) | async-done | bytes 131104 | tf_op jit(solution)/shard_map/all_to_all | solution.py:17
  103.9 0.2 fusion.12
  104.2 14.4 %all_to_all.64 = f32[64,2,128]{2,1,0:T(2,128)S(1)} all-to-all(f32[64,2,128]{2,1,0:T(2,128)S(1)} %copy.129), channel_id=1, replica_groups=mesh['req'=64,'ch'=8] {'req'}, dimensions={0} | all-to-all | bytes 131072 | tf_op jit(solution)/shard_map/all_to_all | solution.py:21
  118.6 9.5 %all_to_all.65 = f32[8,8,2,128]{3,1,2,0:T(8,128)S(1)} all-to-all(f32[8,8,2,128]{3,1,2,0:T(8,128)S(1)} %copy.130), channel_id=1, replica_groups=mesh['req'=64,'ch'=8] {'ch'}, dimensions={0} | all-to-all | bytes 131072 | tf_op jit(solution)/shard_map/all_to_all | solution.py:21
  128.2 0.6 copy-done.4
  128.9 15.4 %all_to_all.66 = bf16[64,2,512]{2,1,0:T(2,128)(2,1)S(1)} all-to-all(bf16[64,2,512]{2,1,0:T(2,128)(2,1)S(1)} %broadcast_in_dim.30), channel_id=1, replica_groups=mesh['req'=64,'ch'=8] {'req'}, dimensions={0} | all-to-all | bytes 262144 | tf_op jit(solution)/shard_map/all_to_all | solution.py:17
  144.4 0.2 multiply_reduce_fusion
  144.7 0.1 copy.133
  144.8 0.1 copy.134
  145.0 0.6 copy-done.6
  145.6 0.2 convolution_convert_fusion.1
  145.9 10.7 %all_to_all.67 = bf16[8,16,386]{2,1,0:T(8,128)(2,1)S(1)} all-to-all(bf16[8,16,386]{2,1,0:T(8,128)(2,1)S(1)} %pad_maximum_fusion), channel_id=1, replica_groups=mesh['req'=64,'ch'=8] {'ch'}, dimensions={0} | all-to-all | bytes 197632 | tf_op jit(solution)/shard_map/all_to_all | solution.py:21
  156.7 0.2 fusion.38
  157.0 9.7 %all_to_all.68 = bf16[8,16,192]{2,1,0:T(8,128)(2,1)S(1)} all-to-all(bf16[8,16,192]{2,1,0:T(8,128)(2,1)S(1)} %broadcast_in_dim.31), channel_id=1, replica_groups=mesh['req'=64,'ch'=8] {'ch'}, dimensions={0} | all-to-all | bytes 98304 | tf_op jit(solution)/shard_map/all_to_all | solution.py:17
  166.7 0.2 convolution_convert_fusion
  166.9 17.3 %all_to_all.69 = bf16[64,2,512]{2,1,0:T(2,128)(2,1)S(1)} all-to-all(bf16[64,2,512]{2,1,0:T(2,128)(2,1)S(1)} %reshape.171), channel_id=1, replica_groups=mesh['req'=64,'ch'=8] {'req'}, dimensions={0} | all-to-all | bytes 262144 | tf_op jit(solution)/shard_map/all_to_all | solution.py:21
  184.2 0.1 convert_reduce_fusion
  184.3 0.6 add_convert_fusion
  (57 shorter events, 2.1 us)
Async XLA Ops:
  0.6 144.4 %copy-start = (bf16[512,384]{1,0:T(8,128)(2,1)S(1)}, bf16[512,384]{1,0:T(8,128)(2,1)}, u32[]{:S(2)}) copy-start(bf16[512,384]{1,0:T(8,128)(2,1)} %param.20) | copy-start | bytes 1179652
  26.5 0.8 copy-start.8
  26.6 0.7 copy-start.9
  26.6 0.7 copy-start.10
  27.5 29.9 %copy-start.2 = (bf16[2,2,32,2048]{3,2,1,0:T(8,128)(2,1)S(1)}, bf16[2,2,32,2048]{3,2,1,0:T(8,128)(2,1)}, u32[]{:S(2)}) copy-start(bf16[2,2,32,2048]{3,2,1,0:T(8,128)(2,1)} %param.15) | copy-start | bytes 1572868
  56.4 0.5 copy-start.5
  58.7 3.6 %copy-start.11 = (s32[2]{0:T(128)S(1)}, s32[2]{0:T(128)}, u32[]{:S(2)}) copy-start(s32[2]{0:T(128)} %param.17) | copy-start | bytes 28
  58.7 13.5 %all-to-all-start.3 = ((f32[8,2,2,2049]{3,2,1,0:T(2,128)}), f32[8,2,2,2049]{3,2,1,0:T(2,128)S(1)}, u32[]{:S(2)}, u32[]{:S(2)}) async-start(f32[8,2,2,2049]{3,2,1,0:T(2,128)} %maximum_bitcast_fusion), calls=%async_computation.3 | async-start | bytes 557056 | tf_op jit(solution)/shard_map/all_to_all | solution.py:21
  62.2 0.7 copy-start.7
  85.7 7.8 %copy-start.3 = (bf16[512,64]{0,1:T(8,128)(2,1)S(1)}, bf16[512,64]{0,1:T(8,128)(2,1)}, u32[]{:S(2)}) copy-start(bf16[512,64]{0,1:T(8,128)(2,1)} %param.18) | copy-start | bytes 196612
  85.7 18.3 %all-to-all-start.5 = ((bf16[64,2,512]{2,1,0:T(2,128)(2,1)}), bf16[64,2,512]{2,1,0:T(2,128)(2,1)S(1)}, u32[]{:S(2)}, u32[]{:S(2)}) async-start(bf16[64,2,512]{2,1,0:T(2,128)(2,1)} %broadcast_in_dim.29), calls=%async_computation.5 | async-start | bytes 262144 | tf_op jit(solution)/shard_map/all_to_all | solution.py:17
  128.1 0.7 copy-start.4
  144.9 0.7 copy-start.6
  156.6 10.0 %copy-start.1 = (bf16[192,512]{1,0:T(8,128)(2,1)S(1)}, bf16[192,512]{1,0:T(8,128)(2,1)}, u32[]{:S(2)}) copy-start(bf16[192,512]{1,0:T(8,128)(2,1)} %param.21) | copy-start | bytes 589828

commit v6 on v5

--- a/solution.py
+++ b/solution.py
@@ -44,7 +44,14 @@
     per_ch = n_req // n_ch
     factor = 1.0 / math.sqrt(HD)
 
-    tok_all = gather_rows(tokens, "req", n_req).reshape(total_rows, feat)
+    slot_index = jnp.arange(window, dtype=jnp.int32)
+    offset = (write_pos[:, None] - 1 - slot_index[None, :]) % window
+    usable = offset < lengths[:, None]
+    tok_bcast = jnp.broadcast_to(tokens[None], (n_req,) + tokens.shape)
+    tok_bcast, usable = lax.optimization_barrier((tok_bcast, usable))
+    tokens_wide = tok_bcast[0].astype(jnp.float32)
+
+    tok_all = exchange(tok_bcast, "req").reshape(total_rows, feat)
     wide = tok_all.astype(jnp.float32)
     squares = jnp.sum(wide * wide, axis=1)
     scaled = (wide * attn_gain[None, :]).astype(jnp.bfloat16)
@@ -77,9 +84,6 @@
     full = jnp.sum(exchange(both, "ch"), axis=0)
     scores = full[..., :window] * factor
     own_score = full[..., window] * factor
-    slot_index = jnp.arange(window, dtype=jnp.int32)
-    offset = (write_pos[:, None] - 1 - slot_index[None, :]) % window
-    usable = offset < lengths[:, None]
     scores = jnp.where(usable[:, None, :], scores, -jnp.inf)
     top = jnp.maximum(jnp.max(scores, axis=-1), own_score)
     weights = jnp.exp(scores - top[..., None])
@@ -114,13 +118,13 @@
     attn_all = gather_rows(attn_local, "req", n_req).reshape(total_rows, H * chan)
     ocols = w_out.shape[1]
     lanes = max(ocols, 128)
-    w_out_wide = jnp.pad(w_out, ((0, 0), (0, lanes - ocols)))
-    out_parts = jnp.dot(attn_all, w_out_wide, preferred_element_type=jnp.float32)
+    out_parts = jnp.dot(attn_all, w_out, preferred_element_type=jnp.float32)
+    out_parts = jnp.pad(out_parts, ((0, 0), (0, lanes - ocols)))
     out_parts = exchange(out_parts.reshape(n_req, rows, lanes), "req")
     out_parts = exchange(out_parts.reshape(n_ch, per_ch, rows, lanes), "ch")
     out_sum = jnp.sum(out_parts, axis=0)[..., :ocols]
     out_sum = out_sum.transpose(1, 0, 2).reshape(rows, per_ch * ocols)
-    first = (tokens.astype(jnp.float32) + out_sum).astype(jnp.bfloat16)
+    first = (tokens_wide + out_sum).astype(jnp.bfloat16)
 
     first_all = gather_rows(first, "req", n_req).reshape(total_rows, feat)
     wide2 = first_all.astype(jnp.float32)
@@ -141,10 +145,12 @@
     hidden = (jax.nn.gelu(gate, approximate=True) * up).astype(jnp.bfloat16)
     hidden_all = gather_rows(hidden, "ch", n_ch).reshape(total_rows, hidden_cols)
     down = jnp.dot(hidden_all, w_down, preferred_element_type=jnp.float32)
-    down = exchange(down.astype(jnp.bfloat16).reshape(n_req, rows, down.shape[1]), "req")
-    down = jnp.sum(down.astype(jnp.float32), axis=0)
-    layer_out = (first.astype(jnp.float32) + down).astype(jnp.bfloat16)
-    return (layer_out, keyval_new)
+    down_payload = down.astype(jnp.bfloat16).reshape(n_req, rows, down.shape[1])
+    down_payload, first_wide = lax.optimization_barrier((down_payload, first.astype(jnp.float32)))
+    down = jnp.sum(exchange(down_payload, "req").astype(jnp.float32), axis=0)
+    layer_out = (first_wide + down).astype(jnp.bfloat16)
+    layer_out, keyval_out = lax.optimization_barrier((layer_out, keyval_new))
+    return (layer_out, keyval_out)
 
 
 def solution(mesh):

time: 186 us -> 186 us (level)
  blocking collectives: 141 us -> 151 us
  starting transfers between devices: 11.4 us -> 6.72 us
  waiting for transfers between devices: 19.4 us -> 15.3 us
    all_to_all x6 -> x7, blocking collectives: 80.1 us -> 107 us  [exchange(): return lax.all_to_all(x, axis, 0, 0)]
    all_to_all x4 -> x3, blocking collectives: 61.2 us -> 44.1 us  [gather_rows(): return lax.all_to_all(jnp.broadcast_to(x[None], (n,) + x.shape), axis, 0, 0)]
    all_to_all x1, starting transfers between devices: 7.83 us -> 3.35 us  [gather_rows(): return lax.all_to_all(jnp.broadcast_to(x[None], (n,) + x.shape), axis, 0, 0)]
    all_to_all x1, waiting for transfers between devices: 10.3 us -> 7.23 us  [gather_rows(): return lax.all_to_all(jnp.broadcast_to(x[None], (n,) + x.shape), axis, 0, 0)]
where the time goes in v6:
time: 186 us
  blocking collectives  151 us (81%)
  waiting for transfers between devices  15.3 us (8%)
  starting transfers between devices  6.72 us (4%)
  local copies, waits for them, and re-layouts  6.44 us (3%)
  other arithmetic  4.22 us (2%)
    all_to_all x7, blocking collectives, exchange(): return lax.all_to_all(x, axis, 0, 0)  107 us
    all_to_all x3, blocking collectives, gather_rows(): return lax.all_to_all(jnp.broadcast_to(x[None], (n,) + x.shape), axis, 0, 0)  44.1 us
    all_to_all x1, waiting for transfers between devices, exchange(): return lax.all_to_all(x, axis, 0, 0)  8.08 us
    all_to_all x1, waiting for transfers between devices, gather_rows(): return lax.all_to_all(jnp.broadcast_to(x[None], (n,) + x.shape), axis, 0, 0)  7.23 us
  transfers between devices with their start and end apart: 2, of which 2 were waited for; matrix products, arithmetic and copies ran while one was open for 0% of the time, Pallas kernels for 0%

profile of v6, /device:TPU:1, one launch (start us, length us, event | category | flops | bytes accessed | tf_op | source)
XLA Modules:
  0.0 185.6 jit_solution(4064421364552890449)
XLA Ops:
  0.7 0.7 broadcast_add_fusion
  1.4 0.1 fusion.30
  1.5 0.6 copy-done.5
  2.1 25.0 %all_to_all.60 = bf16[64,2,512]{2,1,0:T(2,128)(2,1)S(1)} all-to-all(bf16[64,2,512]{2,1,0:T(2,128)(2,1)S(1)} %broadcast_in_dim.26), channel_id=1, replica_groups=mesh['req'=64,'ch'=8] {'req'}, dimensions={0} | all-to-all | bytes 262144 | tf_op jit(solution)/shard_map/all_to_all | solution.py:21
  27.1 0.1 fusion.3
  27.3 0.5 copy.138
  27.8 0.2 copy-done.8
  28.0 0.2 fusion.9
  28.4 14.4 %all_to_all.61 = f32[64,2,73]{2,1,0:T(2,128)S(1)} all-to-all(f32[64,2,73]{2,1,0:T(2,128)S(1)} %copy.139), channel_id=1, replica_groups=mesh['req'=64,'ch'=8] {'req'}, dimensions={0} | all-to-all | bytes 74752 | tf_op jit(solution)/shard_map/all_to_all | solution.py:21
  42.8 13.8 %all_to_all.62 = f32[8,8,2,73]{3,1,2,0:T(8,128)S(1)} all-to-all(f32[8,8,2,73]{3,1,2,0:T(8,128)S(1)} %copy.140), channel_id=1, replica_groups=mesh['req'=64,'ch'=8] {'ch'}, dimensions={0} | all-to-all | bytes 74752 | tf_op jit(solution)/shard_map/all_to_all | solution.py:21
  56.7 0.2 fusion.42
  57.1 0.4 copy-done.4
  57.7 0.2 multiply_reduce_fusion.1
  57.9 0.2 copy.142
  58.1 0.2 fusion.5
  58.3 0.1 concatenate.29
  58.5 0.1 maximum_bitcast_fusion
  58.6 12.3 %all_to_all.63 = f32[8,2,2,2049]{3,2,1,0:T(2,128)S(1)} all-to-all(f32[8,2,2,2049]{3,2,1,0:T(2,128)S(1)} %maximum_bitcast_fusion), channel_id=1, replica_groups=mesh['req'=64,'ch'=8] {'ch'}, dimensions={0} | all-to-all | bytes 524544 | tf_op jit(solution)/shard_map/all_to_all | solution.py:21
  71.0 0.1 fusion.47
  71.2 0.2 fusion.18
  71.4 0.1 copy.147
  71.6 0.1 copy.146
  71.7 0.1 copy.145
  72.0 11.3 %all_to_all.64 = bf16[8,2,2,2051]{3,2,1,0:T(2,128)(2,1)S(1)} all-to-all(bf16[8,2,2,2051]{3,2,1,0:T(2,128)(2,1)S(1)} %broadcast_in_dim.29), channel_id=1, replica_groups=mesh['req'=64,'ch'=8] {'ch'}, dimensions={0} | all-to-all | bytes 262528 | tf_op jit(solution)/shard_map/all_to_all | solution.py:17
  83.5 0.1 convert_reduce_fusion.2
  83.6 0.2 fusion.1
  84.0 17.3 %all_to_all.65 = bf16[64,2,512]{2,1,0:T(2,128)(2,1)S(1)} all-to-all(bf16[64,2,512]{2,1,0:T(2,128)(2,1)S(1)} %broadcast_in_dim.31), channel_id=1, replica_groups=mesh['req'=64,'ch'=8] {'req'}, dimensions={0} | all-to-all | bytes 262144 | tf_op jit(solution)/shard_map/all_to_all | solution.py:17
  101.4 0.8 copy-done.3
  102.2 0.2 fusion.48
  102.4 14.4 %all_to_all.66 = f32[64,2,128]{2,1,0:T(2,128)S(1)} all-to-all(f32[64,2,128]{2,1,0:T(2,128)S(1)} %bitcast.64), channel_id=1, replica_groups=mesh['req'=64,'ch'=8] {'req'}, dimensions={0} | all-to-all | bytes 131072 | tf_op jit(solution)/shard_map/all_to_all | solution.py:21
  116.8 9.5 %all_to_all.67 = f32[8,8,2,128]{3,2,1,0:T(2,128)S(1)} all-to-all(f32[8,8,2,128]{3,2,1,0:T(2,128)S(1)} %bitcast.65), channel_id=1, replica_groups=mesh['req'=64,'ch'=8] {'ch'}, dimensions={0} | all-to-all | bytes 131072 | tf_op jit(solution)/shard_map/all_to_all | solution.py:21
  126.5 15.4 %all_to_all.68 = bf16[64,2,512]{2,1,0:T(2,128)(2,1)S(1)} all-to-all(bf16[64,2,512]{2,1,0:T(2,128)(2,1)S(1)} %broadcast_in_dim.33), channel_id=1, replica_groups=mesh['req'=64,'ch'=8] {'req'}, dimensions={0} | all-to-all | bytes 262144 | tf_op jit(solution)/shard_map/all_to_all | solution.py:17
  142.0 0.2 multiply_reduce_fusion
  142.3 0.1 copy.154
  142.4 0.1 copy.153
  142.6 0.6 copy-done.6
  143.2 0.2 convolution_convert_fusion.1
  143.5 0.7 pad_maximum_fusion
  144.2 3.4 %all-to-all-start.9 = ((bf16[8,16,386]{2,1,0:T(8,128)(2,1)}), bf16[8,16,386]{2,1,0:T(8,128)(2,1)S(1)}, u32[]{:S(2)}, u32[]{:S(2)}) async-start(bf16[8,16,386]{2,1,0:T(8,128)(2,1)} %pad_maximum_fusion), calls=%async_computation.9 | async-start | bytes 262144 | tf_op jit(solution)/shard_map/all_to_all | solution.py:21
  147.6 8.1 %all-to-all-done.9 = bf16[8,16,386]{2,1,0:T(8,128)(2,1)S(1)} async-done(((bf16[8,16,386]{2,1,0:T(8,128)(2,1)}), bf16[8,16,386]{2,1,0:T(8,128)(2,1)S(1)}, u32[]{:S(2)}, u32[]{:S(2)}) %all-to-all-start.9) | async-done | bytes 98848 | tf_op jit(solution)/shard_map/all_to_all | solution.py:21
  155.7 0.2 fusion.34
  156.0 0.6 broadcast_in_dim.34
  156.7 3.3 %all-to-all-start.10 = ((bf16[8,16,192]{2,1,0:T(8,128)(2,1)}), bf16[8,16,192]{2,1,0:T(8,128)(2,1)S(1)}, u32[]{:S(2)}, u32[]{:S(2)}) async-start(bf16[8,16,192]{2,1,0:T(8,128)(2,1)} %broadcast_in_dim.34), calls=%async_computation.10 | async-start | bytes 131072 | tf_op jit(solution)/shard_map/all_to_all | solution.py:17
  160.0 7.2 %all-to-all-done.10 = bf16[8,16,192]{2,1,0:T(8,128)(2,1)S(1)} async-done(((bf16[8,16,192]{2,1,0:T(8,128)(2,1)}), bf16[8,16,192]{2,1,0:T(8,128)(2,1)S(1)}, u32[]{:S(2)}, u32[]{:S(2)}) %all-to-all-start.10) | async-done | bytes 49184 | tf_op jit(solution)/shard_map/all_to_all | solution.py:17
  167.3 0.2 convolution_convert_fusion
  167.5 17.3 %all_to_all.69 = bf16[64,2,512]{2,1,0:T(2,128)(2,1)S(1)} all-to-all(bf16[64,2,512]{2,1,0:T(2,128)(2,1)S(1)} %reshape.142), channel_id=1, replica_groups=mesh['req'=64,'ch'=8] {'req'}, dimensions={0} | all-to-all | bytes 262144 | tf_op jit(solution)/shard_map/all_to_all | solution.py:21
  184.8 0.1 convert_reduce_fusion
  185.0 0.6 add_convert_fusion
  (57 shorter events, 2.2 us)
Async XLA Ops:
  0.6 142.0 %copy-start = (bf16[512,384]{1,0:T(8,128)(2,1)S(1)}, bf16[512,384]{1,0:T(8,128)(2,1)}, u32[]{:S(2)}) copy-start(bf16[512,384]{1,0:T(8,128)(2,1)} %param.20) | copy-start | bytes 1179652
  0.6 0.7 copy-start.7
  1.4 0.7 copy-start.5
  27.2 0.8 copy-start.8
  27.3 0.7 copy-start.9
  27.3 0.7 copy-start.10
  28.2 29.9 %copy-start.2 = (bf16[2,2,32,2048]{3,2,1,0:T(8,128)(2,1)S(1)}, bf16[2,2,32,2048]{3,2,1,0:T(8,128)(2,1)}, u32[]{:S(2)}) copy-start(bf16[2,2,32,2048]{3,2,1,0:T(8,128)(2,1)} %param.15) | copy-start | bytes 1572868
  57.1 0.5 copy-start.4
  101.4 0.8 copy-start.3
  142.5 0.7 copy-start.6
  144.2 11.5 %all-to-all-start.9 = ((bf16[8,16,386]{2,1,0:T(8,128)(2,1)}), bf16[8,16,386]{2,1,0:T(8,128)(2,1)S(1)}, u32[]{:S(2)}, u32[]{:S(2)}) async-start(bf16[8,16,386]{2,1,0:T(8,128)(2,1)} %pad_maximum_fusion), calls=%async_computation.9 | async-start | bytes 262144 | tf_op jit(solution)/shard_map/all_to_all | solution.py:21
  147.6 19.6 %copy-start.1 = (bf16[192,512]{1,0:T(8,128)(2,1)S(1)}, bf16[192,512]{1,0:T(8,128)(2,1)}, u32[]{:S(2)}) copy-start(bf16[192,512]{1,0:T(8,128)(2,1)} %param.21) | copy-start | bytes 589828
  156.7 10.6 %all-to-all-start.10 = ((bf16[8,16,192]{2,1,0:T(8,128)(2,1)}), bf16[8,16,192]{2,1,0:T(8,128)(2,1)S(1)}, u32[]{:S(2)}, u32[]{:S(2)}) async-start(bf16[8,16,192]{2,1,0:T(8,128)(2,1)} %broadcast_in_dim.34), calls=%async_computation.10 | async-start | bytes 131072 | tf_op jit(solution)/shard_map/all_to_all | solution.py:17

commit v7 on v6

--- a/solution.py
+++ b/solution.py
@@ -55,12 +55,14 @@
     wide = tok_all.astype(jnp.float32)
     squares = jnp.sum(wide * wide, axis=1)
     scaled = (wide * attn_gain[None, :]).astype(jnp.bfloat16)
-    joined = jnp.concatenate([w_query, w_keyval], axis=1)
     qcols = w_query.shape[1]
     kcols = w_keyval.shape[1]
+    spare = jnp.zeros((w_query.shape[0], 1), w_query.dtype)
+    joined = jnp.concatenate([w_query, w_keyval, spare], axis=1)
     parts = jnp.dot(scaled, joined, preferred_element_type=jnp.float32)
-    parts = jnp.concatenate([parts, squares[:, None]], axis=1)
     width = parts.shape[1]
+    is_sq = jnp.arange(width, dtype=jnp.int32)[None, :] == width - 1
+    parts = jnp.where(is_sq, squares[:, None], parts)
     parts = exchange(parts.reshape(n_req, rows, width), "req")
     parts = exchange(parts.reshape(n_ch, per_ch, rows, width), "ch")
     summed = jnp.sum(parts, axis=0)
@@ -145,12 +147,10 @@
     hidden = (jax.nn.gelu(gate, approximate=True) * up).astype(jnp.bfloat16)
     hidden_all = gather_rows(hidden, "ch", n_ch).reshape(total_rows, hidden_cols)
     down = jnp.dot(hidden_all, w_down, preferred_element_type=jnp.float32)
-    down_payload = down.astype(jnp.bfloat16).reshape(n_req, rows, down.shape[1])
-    down_payload, first_wide = lax.optimization_barrier((down_payload, first.astype(jnp.float32)))
-    down = jnp.sum(exchange(down_payload, "req").astype(jnp.float32), axis=0)
-    layer_out = (first_wide + down).astype(jnp.bfloat16)
-    layer_out, keyval_out = lax.optimization_barrier((layer_out, keyval_new))
-    return (layer_out, keyval_out)
+    down = exchange(down.astype(jnp.bfloat16).reshape(n_req, rows, down.shape[1]), "req")
+    down = jnp.sum(down.astype(jnp.float32), axis=0)
+    layer_out = (first.astype(jnp.float32) + down).astype(jnp.bfloat16)
+    return (layer_out, keyval_new)
 
 
 def solution(mesh):

time: 186 us -> 187 us (level)
  blocking collectives: 151 us -> 129 us
  starting transfers between devices: 6.72 us -> 21.9 us
  waiting for transfers between devices: 15.3 us -> 20.5 us
    all_to_all x7 -> x6, blocking collectives: 107 us -> 75.2 us  [exchange(): return lax.all_to_all(x, axis, 0, 0)]
    all_to_all x1 -> x2, starting transfers between devices: 3.37 us -> 21.9 us  [exchange(): return lax.all_to_all(x, axis, 0, 0)]
    all_to_all x1 -> x2, waiting for transfers between devices: 8.08 us -> 20.5 us  [exchange(): return lax.all_to_all(x, axis, 0, 0)]
    all_to_all x3 -> x4, blocking collectives: 44.1 us -> 53.8 us  [gather_rows(): return lax.all_to_all(jnp.broadcast_to(x[None], (n,) + x.shape), axis, 0, 0)]
    all_to_all x1 -> x0, waiting for transfers between devices: 7.23 us -> none  [gather_rows(): return lax.all_to_all(jnp.broadcast_to(x[None], (n,) + x.shape), axis, 0, 0)]
    all_to_all x1 -> x0, starting transfers between devices: 3.35 us -> none  [gather_rows(): return lax.all_to_all(jnp.broadcast_to(x[None], (n,) + x.shape), axis, 0, 0)]
where the time goes in v7:
time: 187 us; the launch traced here: 186 us
  blocking collectives  129 us (69%)
  starting transfers between devices  21.9 us (12%)
  waiting for transfers between devices  20.5 us (11%)
  local copies, waits for them, and re-layouts  7.36 us (4%)
  other arithmetic  4.99 us (3%)
    all_to_all x6, blocking collectives, exchange(): return lax.all_to_all(x, axis, 0, 0)  75.2 us
    all_to_all x4, blocking collectives, gather_rows(): return lax.all_to_all(jnp.broadcast_to(x[None], (n,) + x.shape), axis, 0, 0)  53.8 us
    all_to_all x2, starting transfers between devices, exchange(): return lax.all_to_all(x, axis, 0, 0)  21.9 us
    all_to_all x2, waiting for transfers between devices, exchange(): return lax.all_to_all(x, axis, 0, 0)  20.5 us
  transfers between devices with their start and end apart: 2, of which 2 were waited for; matrix products, arithmetic and copies ran while one was open for 0% of the time, Pallas kernels for 0%

profile of v7, /device:TPU:1, one launch (start us, length us, event | category | flops | bytes accessed | tf_op | source)
XLA Modules:
  0.0 185.8 jit_solution(1178562708264305200)
XLA Ops:
  0.7 0.7 broadcast_add_fusion
  1.5 0.6 copy-done.5
  2.1 0.7 broadcast_in_dim.46
  2.8 14.8 %all-to-all-start = ((bf16[64,2,512]{2,1,0:T(2,128)(2,1)}), bf16[64,2,512]{2,1,0:T(2,128)(2,1)S(1)}, u32[]{:S(2)}, u32[]{:S(2)}) async-start(bf16[64,2,512]{2,1,0:T(2,128)(2,1)} %broadcast_in_dim.46), calls=%async_computation | async-start | bytes 262144 | tf_op jit(solution)/shard_map/all_to_all | solution.py:21
  17.7 10.3 %all-to-all-done = bf16[64,2,512]{2,1,0:T(2,128)(2,1)S(1)} async-done(((bf16[64,2,512]{2,1,0:T(2,128)(2,1)}), bf16[64,2,512]{2,1,0:T(2,128)(2,1)S(1)}, u32[]{:S(2)}, u32[]{:S(2)}) %all-to-all-start) | async-done | bytes 131104 | tf_op jit(solution)/shard_map/all_to_all | solution.py:21
  27.9 0.2 multiply_reduce_fusion.1
  28.1 0.1 broadcast_in_dim.49
  28.4 0.8 copy-done.8
  29.1 0.2 convolution_select_fusion
  29.4 14.4 %all_to_all.60 = f32[64,2,73]{2,1,0:T(2,128)S(1)} all-to-all(f32[64,2,73]{2,1,0:T(2,128)S(1)} %bitcast.64), channel_id=1, replica_groups=mesh['req'=64,'ch'=8] {'req'}, dimensions={0} | all-to-all | bytes 74752 | tf_op jit(solution)/shard_map/all_to_all | solution.py:21
  43.9 13.8 %all_to_all.61 = f32[8,8,2,73]{3,2,1,0:T(2,128)S(1)} all-to-all(f32[8,8,2,73]{3,2,1,0:T(2,128)S(1)} %bitcast.61), channel_id=1, replica_groups=mesh['req'=64,'ch'=8] {'ch'}, dimensions={0} | all-to-all | bytes 74752 | tf_op jit(solution)/shard_map/all_to_all | solution.py:21
  57.8 0.2 fusion.39
  58.3 0.4 copy-done.4
  58.8 0.2 multiply_reduce_fusion.2
  59.0 0.2 copy.85
  59.2 0.2 fusion.3
  59.5 0.1 concatenate.21
  59.6 0.1 maximum_bitcast_fusion
  59.8 12.3 %all_to_all.62 = f32[8,2,2,2049]{3,2,1,0:T(2,128)S(1)} all-to-all(f32[8,2,2,2049]{3,2,1,0:T(2,128)S(1)} %maximum_bitcast_fusion), channel_id=1, replica_groups=mesh['req'=64,'ch'=8] {'ch'}, dimensions={0} | all-to-all | bytes 524544 | tf_op jit(solution)/shard_map/all_to_all | solution.py:21
  72.1 0.1 fusion.44
  72.4 0.2 fusion.16
  72.6 0.1 copy.90
  72.7 0.1 copy.89
  72.8 0.1 copy.88
  73.1 11.3 %all_to_all.63 = bf16[8,2,2,2051]{3,2,1,0:T(2,128)(2,1)S(1)} all-to-all(bf16[8,2,2,2051]{3,2,1,0:T(2,128)(2,1)S(1)} %broadcast_in_dim.53), channel_id=1, replica_groups=mesh['req'=64,'ch'=8] {'ch'}, dimensions={0} | all-to-all | bytes 262528 | tf_op jit(solution)/shard_map/all_to_all | solution.py:17
  84.6 0.1 convert_reduce_fusion.2
  84.7 0.2 fusion.1
  85.1 17.3 %all_to_all.64 = bf16[64,2,512]{2,1,0:T(2,128)(2,1)S(1)} all-to-all(bf16[64,2,512]{2,1,0:T(2,128)(2,1)S(1)} %broadcast_in_dim.55), channel_id=1, replica_groups=mesh['req'=64,'ch'=8] {'req'}, dimensions={0} | all-to-all | bytes 262144 | tf_op jit(solution)/shard_map/all_to_all | solution.py:17
  102.5 0.8 copy-done.3
  103.3 0.2 fusion.45
  103.5 14.4 %all_to_all.65 = f32[64,2,128]{2,1,0:T(2,128)S(1)} all-to-all(f32[64,2,128]{2,1,0:T(2,128)S(1)} %bitcast.62), channel_id=1, replica_groups=mesh['req'=64,'ch'=8] {'req'}, dimensions={0} | all-to-all | bytes 131072 | tf_op jit(solution)/shard_map/all_to_all | solution.py:21
  117.9 9.5 %all_to_all.66 = f32[8,8,2,128]{3,2,1,0:T(2,128)S(1)} all-to-all(f32[8,8,2,128]{3,2,1,0:T(2,128)S(1)} %bitcast.63), channel_id=1, replica_groups=mesh['req'=64,'ch'=8] {'ch'}, dimensions={0} | all-to-all | bytes 131072 | tf_op jit(solution)/shard_map/all_to_all | solution.py:21
  127.6 0.7 fusion.36
  128.3 15.4 %all_to_all.67 = bf16[64,2,512]{2,1,0:T(2,128)(2,1)S(1)} all-to-all(bf16[64,2,512]{2,1,0:T(2,128)(2,1)S(1)} %broadcast_in_dim.57), channel_id=1, replica_groups=mesh['req'=64,'ch'=8] {'req'}, dimensions={0} | all-to-all | bytes 262144 | tf_op jit(solution)/shard_map/all_to_all | solution.py:17
  143.8 0.2 multiply_reduce_fusion
  144.1 0.1 copy.98
  144.2 0.1 copy.97
  144.4 0.6 copy-done.6
  145.0 0.2 convolution_convert_fusion.1
  145.3 10.7 %all_to_all.68 = bf16[8,16,386]{2,1,0:T(8,128)(2,1)S(1)} all-to-all(bf16[8,16,386]{2,1,0:T(8,128)(2,1)S(1)} %pad_maximum_fusion), channel_id=1, replica_groups=mesh['req'=64,'ch'=8] {'ch'}, dimensions={0} | all-to-all | bytes 197632 | tf_op jit(solution)/shard_map/all_to_all | solution.py:21
  156.1 0.2 fusion.32
  156.4 9.7 %all_to_all.69 = bf16[8,16,192]{2,1,0:T(8,128)(2,1)S(1)} all-to-all(bf16[8,16,192]{2,1,0:T(8,128)(2,1)S(1)} %broadcast_in_dim.58), channel_id=1, replica_groups=mesh['req'=64,'ch'=8] {'ch'}, dimensions={0} | all-to-all | bytes 98304 | tf_op jit(solution)/shard_map/all_to_all | solution.py:17
  166.1 0.2 convolution_convert_fusion
  166.3 0.7 reshape.146
  167.0 7.1 %all-to-all-start.11 = ((bf16[64,2,512]{2,1,0:T(2,128)(2,1)}), bf16[64,2,512]{2,1,0:T(2,128)(2,1)S(1)}, u32[]{:S(2)}, u32[]{:S(2)}) async-start(bf16[64,2,512]{2,1,0:T(2,128)(2,1)} %reshape.146), calls=%async_computation.11 | async-start | bytes 262144 | tf_op jit(solution)/shard_map/all_to_all | solution.py:21
  174.2 10.3 %all-to-all-done.11 = bf16[64,2,512]{2,1,0:T(2,128)(2,1)S(1)} async-done(((bf16[64,2,512]{2,1,0:T(2,128)(2,1)}), bf16[64,2,512]{2,1,0:T(2,128)(2,1)S(1)}, u32[]{:S(2)}, u32[]{:S(2)}) %all-to-all-start.11) | async-done | bytes 131104 | tf_op jit(solution)/shard_map/all_to_all | solution.py:21
  184.4 0.1 convert_reduce_fusion
  184.6 1.3 add_convert_fusion
  (58 shorter events, 2.3 us)
Async XLA Ops:
  0.6 143.8 %copy-start = (bf16[512,384]{1,0:T(8,128)(2,1)S(1)}, bf16[512,384]{1,0:T(8,128)(2,1)}, u32[]{:S(2)}) copy-start(bf16[512,384]{1,0:T(8,128)(2,1)} %param.20) | copy-start | bytes 1179652
  0.6 0.7 copy-start.7
  1.4 0.7 copy-start.5
  2.8 25.2 %all-to-all-start = ((bf16[64,2,512]{2,1,0:T(2,128)(2,1)}), bf16[64,2,512]{2,1,0:T(2,128)(2,1)S(1)}, u32[]{:S(2)}, u32[]{:S(2)}) async-start(bf16[64,2,512]{2,1,0:T(2,128)(2,1)} %broadcast_in_dim.46), calls=%async_computation | async-start | bytes 262144 | tf_op jit(solution)/shard_map/all_to_all | solution.py:21
  28.3 0.8 copy-start.8
  28.3 0.8 copy-start.9
  28.3 0.8 copy-start.10
  29.1 30.1 %copy-start.2 = (bf16[2,2,32,2048]{3,2,1,0:T(8,128)(2,1)S(1)}, bf16[2,2,32,2048]{3,2,1,0:T(8,128)(2,1)}, u32[]{:S(2)}) copy-start(bf16[2,2,32,2048]{3,2,1,0:T(8,128)(2,1)} %param.15) | copy-start | bytes 1572868
  58.2 0.5 copy-start.4
  102.5 0.8 copy-start.3
  144.3 0.7 copy-start.6
  156.0 10.0 %copy-start.1 = (bf16[192,512]{1,0:T(8,128)(2,1)S(1)}, bf16[192,512]{1,0:T(8,128)(2,1)}, u32[]{:S(2)}) copy-start(bf16[192,512]{1,0:T(8,128)(2,1)} %param.21) | copy-start | bytes 589828
  167.0 17.5 %all-to-all-start.11 = ((bf16[64,2,512]{2,1,0:T(2,128)(2,1)}), bf16[64,2,512]{2,1,0:T(2,128)(2,1)S(1)}, u32[]{:S(2)}, u32[]{:S(2)}) async-start(bf16[64,2,512]{2,1,0:T(2,128)(2,1)} %reshape.146), calls=%async_computation.11 | async-start | bytes 262144 | tf_op jit(solution)/shard_map/all_to_all | solution.py:21
